TPU v7x, 512 devices: a whole 4x4x16 slice. The times are simulated.
512 devices in a mesh: dp: 32 (over y, x, core), tensor: 16 (over z).
Axes of the slice: x: 4, y: 4, z: 16, core: 2. Of those that a mesh axis runs over, the one named last changes fastest.
Arguments:
- activations: bfloat16 [32768, 4096], P('dp', 'tensor'), may hold values from -40 to 40
- labels: int32 [32768], P('dp'), may hold values from 0 to 7, as said below
Outputs:
- covariance: float32 [4096, 4096], P('tensor', 'dp')
- cross_covariance: float32 [8, 4096], P(None, 'tensor')
Inputs may be any that keep to these rules, and one draw needn't show every extreme that they name: Every one of the 8 classes labels at least one token.
All inputs are finite; a program needn't handle non-finite values.
Results may differ from a plain program's by a relative error of at most 0.0003.
Values may be sent and summed in bfloat16 or wider, within the bound.
No kernel may reach another device: no remote copies, remote signals or barrier semaphores. Data moves between devices by JAX's collectives and lax.ppermute only.
A program may use at most 64 MiB of HBM per device.

v0:
```python
import jax
import jax.numpy as jnp
from jax import lax
from jax.sharding import PartitionSpec as P

D = 4096
CLASSES = 8
CHUNKS = 4
RS_BITS = (0, 1, 3, 2, 4)


def butterfly_sum(x, axis, n):
    k = 1
    while k < n:
        perm = [(i, i ^ k) for i in range(n)]
        x = x + lax.ppermute(x, axis, perm)
        k *= 2
    return x


def butterfly_scatter(x, axis, n, bits):
    me = lax.axis_index(axis)
    nb = len(bits)
    tail = x.shape[1:]
    x = x.reshape((2,) * nb + tail)
    left = list(range(nb))
    for b in bits:
        pos = left.index(nb - 1 - b)
        mine = me >> b & 1
        keep = lax.dynamic_index_in_dim(x, mine, pos, keepdims=False)
        send = lax.dynamic_index_in_dim(x, 1 - mine, pos, keepdims=False)
        perm = [(i, i ^ 1 << b) for i in range(n)]
        x = keep + lax.ppermute(send, axis, perm)
        left.pop(pos)
    return x


def body(activations, labels):
    tok_rows, slice_width = activations.shape
    n_dp = lax.axis_size("dp")
    n_t = lax.axis_size("tensor")
    assert n_dp == 1 << len(RS_BITS)
    token_total = tok_rows * n_dp
    col_width = D // n_dp
    halves = slice_width // col_width
    w = col_width // CHUNKS
    classes = jnp.arange(CLASSES, dtype=jnp.int32)
    matches = labels[None, :] == classes[:, None]
    onehot = matches.astype(jnp.bfloat16)
    local_counts = jnp.sum(matches.astype(jnp.float32), axis=1)
    own_local = jnp.dot(onehot, activations, preferred_element_type=jnp.float32)
    stats = jnp.concatenate(
        [own_local, jnp.broadcast_to(local_counts[:, None], (CLASSES, 128))], axis=1
    )
    stats = butterfly_sum(stats, "dp", n_dp)
    own_sums = stats[:, :slice_width]
    class_counts = stats[:, slice_width]
    own_t = activations.T.reshape(halves, col_width, tok_rows)
    parts = [own_t[:, k * w : (k + 1) * w, :].reshape(halves * w, tok_rows) for k in range(CHUNKS)]
    pieces = []
    colsums = []
    for k in range(CHUNKS):
        part = parts[k]
        g = lax.all_gather(part, "tensor", axis=0, tiled=True)
        prod = lax.dot_general(
            g, activations, (((1,), (0,)), ((), ())), preferred_element_type=jnp.float32
        ).reshape(n_dp, w, slice_width)
        colsums.append(jnp.sum(g.astype(jnp.float32), axis=1).reshape(n_dp, w))
        if k == CHUNKS - 1:
            colsum = jnp.concatenate(colsums, axis=1)
            extra = jnp.zeros((n_dp, 8, slice_width), jnp.float32)
            extra = extra.at[:, 0, :col_width].set(colsum)
            prod = jnp.concatenate([prod, extra], axis=1)
        if k + 1 < CHUNKS:
            parts[k + 1], prod = lax.optimization_barrier((parts[k + 1], prod))
        piece = butterfly_scatter(prod, "dp", n_dp, RS_BITS)
        if k + 2 < CHUNKS:
            parts[k + 2], piece = lax.optimization_barrier((parts[k + 2], piece))
        pieces.append(piece)
    mean_cols = pieces[-1][w, :col_width] / token_total
    gram_cols = jnp.concatenate(pieces[:-1] + [pieces[-1][:w]], axis=0)
    mean_rows = jnp.sum(own_sums, axis=0) / token_total
    covariance = gram_cols.T / token_total - mean_rows[:, None] * mean_cols[None, :]
    cross_covariance = (own_sums - class_counts[:, None] * mean_rows[None, :]) / token_total
    return (covariance, cross_covariance)


def solution(mesh):
    in_specs = (P("dp", "tensor"), P("dp"))
    out_specs = (P("tensor", "dp"), P(None, "tensor"))
    return jax.shard_map(body, mesh=mesh, in_specs=in_specs, out_specs=out_specs, check_vma=False)
```

profile of v0, /device:TPU:32, one launch (start us, length us, event | category | flops | bytes accessed | tf_op | source)
XLA Modules:
  0.0 359.2 jit_solution(11233232944824296545)
XLA Ops:
  7.2 1.3 copy.32
  8.5 0.8 fusion.11
  9.4 78.0 %all-gather.5.cloned.1.call-done = bf16[1024,1024]{1,0:T(8,128)(2,1)} async-done(((bf16[64,1024]{1,0:T(8,128)(2,1)}), bf16[1024,1024]{1,0:T(8,128)(2,1)}) %all-gather.5.cloned.1.call-update) | async-done | bytes 2097168 | tf_op jit(solution)/shard_map/all_gather | solution.py:64
  87.4 2.3 fusion.12
  89.9 1.9 collective-permute-start
  91.9 1.9 collective-permute-done
  93.8 3.4 collective-permute-start.1
  97.2 6.9 %collective-permute-done.1 = f32[2,2,2,32,256]{4,3,2,1,0:T(8,128)S(1)} collective-permute-done((f32[2,2,2,32,256]{4,3,2,1,0:T(8,128)S(1)}, f32[2,2,2,32,256]{4,3,2,1,0:T(8,128)S(1)}, u32[]{:S(2)}, u32[]{:S(2)}) %collective-permute-start.1) | collective-permute-done | bytes 262176 | tf_op jit(solution)/shard_map/ppermute | solution.py:33
  104.1 3.4 collective-permute-start.2
  107.5 3.5 collective-permute-done.2
  111.1 4.9 %collective-permute-start.3 = (f32[2,32,256]{2,1,0:T(8,128)S(1)}, f32[2,32,256]{2,1,0:T(8,128)S(1)}, u32[]{:S(2)}, u32[]{:S(2)}) collective-permute-start(f32[2,32,256]{2,1,0:T(8,128)S(1)} %dynamic-slice_bitcast_fusion.11), channel_id=1, source_target_pairs={{0,64},{16,80},{32,96},{48,112},{64,0},{80,16},{96,32},{112,48},{1... | collective-permute-start | bytes 196616 | tf_op jit(solution)/shard_map/ppermute | solution.py:33
  116.0 2.8 collective-permute-done.3
  118.7 4.9 %collective-permute-start.4 = (f32[32,256]{1,0:T(8,128)S(1)}, f32[32,256]{1,0:T(8,128)S(1)}, u32[]{:S(2)}, u32[]{:S(2)}) collective-permute-start(f32[32,256]{1,0:T(8,128)S(1)} %dynamic-slice_bitcast_fusion.15), channel_id=1, source_target_pairs={{0,256},{16,272},{32,288},{48,304},{64,320},{80,336},{96,352},{112... | collective-permute-start | bytes 98312 | tf_op jit(solution)/shard_map/ppermute | solution.py:33
  123.7 2.4 collective-permute-done.4
  126.1 33.2 %all-gather.7.cloned.1.call-done = bf16[1024,1024]{1,0:T(8,128)(2,1)} async-done(((bf16[64,1024]{1,0:T(8,128)(2,1)}), bf16[1024,1024]{1,0:T(8,128)(2,1)}) %all-gather.7.cloned.1.call-update) | async-done | bytes 2097168 | tf_op jit(solution)/shard_map/all_gather | solution.py:64
  159.3 2.3 fusion.13
  161.8 1.9 collective-permute-start.5
  163.8 1.9 collective-permute-done.5
  165.7 3.4 collective-permute-start.6
  169.1 6.8 %collective-permute-done.6 = f32[2,2,2,32,256]{4,3,2,1,0:T(8,128)S(1)} collective-permute-done((f32[2,2,2,32,256]{4,3,2,1,0:T(8,128)S(1)}, f32[2,2,2,32,256]{4,3,2,1,0:T(8,128)S(1)}, u32[]{:S(2)}, u32[]{:S(2)}) %collective-permute-start.6) | collective-permute-done | bytes 262176 | tf_op jit(solution)/shard_map/ppermute | solution.py:33
  176.0 3.5 collective-permute-start.7
  179.5 3.4 collective-permute-done.7
  183.0 4.9 %collective-permute-start.8 = (f32[2,32,256]{2,1,0:T(8,128)S(1)}, f32[2,32,256]{2,1,0:T(8,128)S(1)}, u32[]{:S(2)}, u32[]{:S(2)}) collective-permute-start(f32[2,32,256]{2,1,0:T(8,128)S(1)} %dynamic-slice_bitcast_fusion.10), channel_id=1, source_target_pairs={{0,64},{16,80},{32,96},{48,112},{64,0},{80,16},{96,32},{112,48},{1... | collective-permute-start | bytes 196616 | tf_op jit(solution)/shard_map/ppermute | solution.py:33
  187.9 2.8 collective-permute-done.8
  190.6 4.9 %collective-permute-start.9 = (f32[32,256]{1,0:T(8,128)S(1)}, f32[32,256]{1,0:T(8,128)S(1)}, u32[]{:S(2)}, u32[]{:S(2)}) collective-permute-start(f32[32,256]{1,0:T(8,128)S(1)} %dynamic-slice_bitcast_fusion.14), channel_id=1, source_target_pairs={{0,256},{16,272},{32,288},{48,304},{64,320},{80,336},{96,352},{112... | collective-permute-start | bytes 98312 | tf_op jit(solution)/shard_map/ppermute | solution.py:33
  195.6 2.4 collective-permute-done.9
  198.0 33.4 %all-gather.9.cloned.1.call-done = bf16[1024,1024]{1,0:T(8,128)(2,1)} async-done(((bf16[64,1024]{1,0:T(8,128)(2,1)}), bf16[1024,1024]{1,0:T(8,128)(2,1)}) %all-gather.9.cloned.1.call-update) | async-done | bytes 2097168 | tf_op jit(solution)/shard_map/all_gather | solution.py:64
  231.3 3.4 fusion.14
  235.1 2.0 collective-permute-start.20
  237.2 1.1 collective-permute-done.20
  238.3 3.4 collective-permute-start.21
  241.7 2.2 collective-permute-done.21
  243.9 4.9 %collective-permute-start.22 = (f32[8,384]{1,0:T(8,128)S(1)}, f32[8,384]{1,0:T(8,128)S(1)}, u32[]{:S(2)}, u32[]{:S(2)}) collective-permute-start(f32[8,384]{1,0:T(8,128)S(1)} %add.185), channel_id=1, source_target_pairs={{0,64},{16,80},{32,96},{48,112},{64,0},{80,16},{96,32},{112,48},{1... | collective-permute-start | bytes 36872 | tf_op jit(solution)/shard_map/ppermute | solution.py:16
  248.8 2.2 collective-permute-done.22
  251.0 3.4 collective-permute-start.23
  254.5 2.1 collective-permute-done.23
  256.6 4.9 %collective-permute-start.24 = (f32[8,384]{1,0:T(8,128)S(1)}, f32[8,384]{1,0:T(8,128)S(1)}, u32[]{:S(2)}, u32[]{:S(2)}) collective-permute-start(f32[8,384]{1,0:T(8,128)S(1)} %add.187), channel_id=1, source_target_pairs={{0,256},{16,272},{32,288},{48,304},{64,320},{80,336},{96,352},{112... | collective-permute-start | bytes 36872 | tf_op jit(solution)/shard_map/ppermute | solution.py:16
  261.5 2.2 collective-permute-done.24
  263.7 0.6 broadcast_multiply_fusion
  264.3 1.3 constant_dynamic-slice_fusion.1
  265.6 0.9 copy.63
  266.5 1.9 collective-permute-start.10
  268.8 1.9 convert_reduce_fusion.2
  270.8 1.9 convert_reduce_fusion.1
  272.9 1.1 fusion.2
  274.0 3.4 collective-permute-start.11
  277.4 27.1 %all-gather.11.cloned.1.call-done = bf16[1024,1024]{1,0:T(8,128)(2,1)} async-done(((bf16[64,1024]{1,0:T(8,128)(2,1)}), bf16[1024,1024]{1,0:T(8,128)(2,1)}) %all-gather.11.cloned.1.call-update) | async-done | bytes 2097168 | tf_op jit(solution)/shard_map/all_gather | solution.py:64
  304.5 2.1 convert_reduce_fusion
  306.8 0.7 fusion.15
  307.8 1.9 collective-permute-start.15
  309.8 0.7 subtract_multiply_fusion
  310.5 1.0 bitcast_add_fusion.2
  311.5 3.4 collective-permute-start.12
  315.0 3.4 collective-permute-start.16
  318.4 0.9 collective-permute-done.12
  319.3 4.9 %collective-permute-start.13 = (f32[2,32,256]{2,1,0:T(8,128)S(1)}, f32[2,32,256]{2,1,0:T(8,128)S(1)}, u32[]{:S(2)}, u32[]{:S(2)}) collective-permute-start(f32[2,32,256]{2,1,0:T(8,128)S(1)} %dynamic-slice_bitcast_fusion.9), channel_id=1, source_target_pairs={{0,64},{16,80},{32,96},{48,112},{64,0},{80,16},{96,32},{112,48},{1... | collective-permute-start | bytes 196616 | tf_op jit(solution)/shard_map/ppermute | solution.py:33
  324.2 3.2 collective-permute-done.16
  327.5 2.5 collective-permute-start.17
  330.2 4.6 %collective-permute-done.17 = f32[2,2,40,256]{3,2,1,0:T(8,128)S(1)} collective-permute-done((f32[2,2,40,256]{3,2,1,0:T(8,128)S(1)}, f32[2,2,40,256]{3,2,1,0:T(8,128)S(1)}, u32[]{:S(2)}, u32[]{:S(2)}) %collective-permute-start.17) | collective-permute-done | bytes 163872 | tf_op jit(solution)/shard_map/ppermute | solution.py:33
  334.8 4.9 %collective-permute-start.18 = (f32[2,40,256]{2,1,0:T(8,128)S(1)}, f32[2,40,256]{2,1,0:T(8,128)S(1)}, u32[]{:S(2)}, u32[]{:S(2)}) collective-permute-start(f32[2,40,256]{2,1,0:T(8,128)S(1)} %dynamic-slice_bitcast_fusion.8), channel_id=1, source_target_pairs={{0,64},{16,80},{32,96},{48,112},{64,0},{80,16},{96,32},{112,48},{1... | collective-permute-start | bytes 245768 | tf_op jit(solution)/shard_map/ppermute | solution.py:33
  339.7 4.6 %collective-permute-start.14 = (f32[32,256]{1,0:T(8,128)S(1)}, f32[32,256]{1,0:T(8,128)S(1)}, u32[]{:S(2)}, u32[]{:S(2)}) collective-permute-start(f32[32,256]{1,0:T(8,128)S(1)} %dynamic-slice_bitcast_fusion.13), channel_id=1, source_target_pairs={{0,256},{16,272},{32,288},{48,304},{64,320},{80,336},{96,352},{112... | collective-permute-start | bytes 98312 | tf_op jit(solution)/shard_map/ppermute | solution.py:33
  344.4 2.9 collective-permute-start.19
  347.4 4.5 %collective-permute-done.19 = f32[40,256]{1,0:T(8,128)S(1)} collective-permute-done((f32[40,256]{1,0:T(8,128)S(1)}, f32[40,256]{1,0:T(8,128)S(1)}, u32[]{:S(2)}, u32[]{:S(2)}) %collective-permute-start.19) | collective-permute-done | bytes 40992 | tf_op jit(solution)/shard_map/ppermute | solution.py:33
  351.9 0.8 copy.41
  (85 shorter events, 3.0 us)
Async XLA Ops:
  7.2 80.2 %copy-start.2 = (bf16[1024,256]{1,0:T(8,128)(2,1)S(1)}, bf16[1024,256]{1,0:T(8,128)(2,1)}, u32[]{:S(2)}) copy-start(bf16[1024,256]{1,0:T(8,128)(2,1)} %param.4) | copy-start | bytes 1572868
  7.2 80.2 %all-gather.5.cloned.1.call-start = ((), (), s32[]{:S(2)}) async-start(), calls=%async_computation | async-start | bytes 2228224 | tf_op jit(solution)/shard_map/all_gather | solution.py:64
  9.3 150.0 %all-gather.7.cloned.1.call-start = ((), (), s32[]{:S(2)}) async-start(), calls=%async_computation.1 | async-start | bytes 2228224 | tf_op jit(solution)/shard_map/all_gather | solution.py:64
  89.7 141.6 %all-gather.9.cloned.1.call-start = ((), (), s32[]{:S(2)}) async-start(), calls=%async_computation.2 | async-start | bytes 2228224 | tf_op jit(solution)/shard_map/all_gather | solution.py:64
  89.9 3.8 %collective-permute-start = (f32[2,2,2,2,32,256]{5,4,2,1,0,3:T(8,128)S(1)}, f32[2,2,2,2,32,256]{5,4,2,1,0,3:T(8,128)S(1)}, u32[]{:S(2)}, u32[]{:S(2)}) collective-permute-start(f32[2,2,2,2,32,256]{5,4,2,1,0,3:T(8,128)S(1)} %bitcast.128), channel_id=1, source_target_pairs={{0,16},{16,0},{32,48},{48,32},{64,80},{80,64},{96,112},{112,96},{1... | collective-permute-start | bytes 1572872 | tf_op jit(solution)/shard_map/ppermute | solution.py:33
  93.8 10.2 %collective-permute-start.1 = (f32[2,2,2,32,256]{4,3,2,1,0:T(8,128)S(1)}, f32[2,2,2,32,256]{4,3,2,1,0:T(8,128)S(1)}, u32[]{:S(2)}, u32[]{:S(2)}) collective-permute-start(f32[2,2,2,32,256]{4,3,2,1,0:T(8,128)S(1)} %dynamic-slice_bitcast_fusion.3), channel_id=1, source_target_pairs={{0,32},{16,48},{32,0},{48,16},{64,96},{80,112},{96,64},{112,80},{1... | collective-permute-start | bytes 786440 | tf_op jit(solution)/shard_map/ppermute | solution.py:33
  104.1 6.9 %collective-permute-start.2 = (f32[2,2,32,256]{3,2,1,0:T(8,128)S(1)}, f32[2,2,32,256]{3,2,1,0:T(8,128)S(1)}, u32[]{:S(2)}, u32[]{:S(2)}) collective-permute-start(f32[2,2,32,256]{3,2,1,0:T(8,128)S(1)} %dynamic-slice_bitcast_fusion.7), channel_id=1, source_target_pairs={{0,128},{16,144},{32,160},{48,176},{64,192},{80,208},{96,224},{112... | collective-permute-start | bytes 393224 | tf_op jit(solution)/shard_map/ppermute | solution.py:33
  111.1 7.7 %collective-permute-start.3 = (f32[2,32,256]{2,1,0:T(8,128)S(1)}, f32[2,32,256]{2,1,0:T(8,128)S(1)}, u32[]{:S(2)}, u32[]{:S(2)}) collective-permute-start(f32[2,32,256]{2,1,0:T(8,128)S(1)} %dynamic-slice_bitcast_fusion.11), channel_id=1, source_target_pairs={{0,64},{16,80},{32,96},{48,112},{64,0},{80,16},{96,32},{112,48},{1... | collective-permute-start | bytes 196616 | tf_op jit(solution)/shard_map/ppermute | solution.py:33
  118.7 7.3 %collective-permute-start.4 = (f32[32,256]{1,0:T(8,128)S(1)}, f32[32,256]{1,0:T(8,128)S(1)}, u32[]{:S(2)}, u32[]{:S(2)}) collective-permute-start(f32[32,256]{1,0:T(8,128)S(1)} %dynamic-slice_bitcast_fusion.15), channel_id=1, source_target_pairs={{0,256},{16,272},{32,288},{48,304},{64,320},{80,336},{96,352},{112... | collective-permute-start | bytes 98312 | tf_op jit(solution)/shard_map/ppermute | solution.py:33
  161.6 142.9 %all-gather.11.cloned.1.call-start = ((), (), s32[]{:S(2)}) async-start(), calls=%async_computation.3 | async-start | bytes 2228224 | tf_op jit(solution)/shard_map/all_gather | solution.py:64
  161.8 3.8 %collective-permute-start.5 = (f32[2,2,2,2,32,256]{5,4,2,1,0,3:T(8,128)S(1)}, f32[2,2,2,2,32,256]{5,4,2,1,0,3:T(8,128)S(1)}, u32[]{:S(2)}, u32[]{:S(2)}) collective-permute-start(f32[2,2,2,2,32,256]{5,4,2,1,0,3:T(8,128)S(1)} %bitcast.129), channel_id=1, source_target_pairs={{0,16},{16,0},{32,48},{48,32},{64,80},{80,64},{96,112},{112,96},{1... | collective-permute-start | bytes 1572872 | tf_op jit(solution)/shard_map/ppermute | solution.py:33
  165.7 10.2 %collective-permute-start.6 = (f32[2,2,2,32,256]{4,3,2,1,0:T(8,128)S(1)}, f32[2,2,2,32,256]{4,3,2,1,0:T(8,128)S(1)}, u32[]{:S(2)}, u32[]{:S(2)}) collective-permute-start(f32[2,2,2,32,256]{4,3,2,1,0:T(8,128)S(1)} %dynamic-slice_bitcast_fusion.2), channel_id=1, source_target_pairs={{0,32},{16,48},{32,0},{48,16},{64,96},{80,112},{96,64},{112,80},{1... | collective-permute-start | bytes 786440 | tf_op jit(solution)/shard_map/ppermute | solution.py:33
  176.0 6.9 %collective-permute-start.7 = (f32[2,2,32,256]{3,2,1,0:T(8,128)S(1)}, f32[2,2,32,256]{3,2,1,0:T(8,128)S(1)}, u32[]{:S(2)}, u32[]{:S(2)}) collective-permute-start(f32[2,2,32,256]{3,2,1,0:T(8,128)S(1)} %dynamic-slice_bitcast_fusion.6), channel_id=1, source_target_pairs={{0,128},{16,144},{32,160},{48,176},{64,192},{80,208},{96,224},{112... | collective-permute-start | bytes 393224 | tf_op jit(solution)/shard_map/ppermute | solution.py:33
  183.0 7.7 %collective-permute-start.8 = (f32[2,32,256]{2,1,0:T(8,128)S(1)}, f32[2,32,256]{2,1,0:T(8,128)S(1)}, u32[]{:S(2)}, u32[]{:S(2)}) collective-permute-start(f32[2,32,256]{2,1,0:T(8,128)S(1)} %dynamic-slice_bitcast_fusion.10), channel_id=1, source_target_pairs={{0,64},{16,80},{32,96},{48,112},{64,0},{80,16},{96,32},{112,48},{1... | collective-permute-start | bytes 196616 | tf_op jit(solution)/shard_map/ppermute | solution.py:33
  190.6 7.3 %collective-permute-start.9 = (f32[32,256]{1,0:T(8,128)S(1)}, f32[32,256]{1,0:T(8,128)S(1)}, u32[]{:S(2)}, u32[]{:S(2)}) collective-permute-start(f32[32,256]{1,0:T(8,128)S(1)} %dynamic-slice_bitcast_fusion.14), channel_id=1, source_target_pairs={{0,256},{16,272},{32,288},{48,304},{64,320},{80,336},{96,352},{112... | collective-permute-start | bytes 98312 | tf_op jit(solution)/shard_map/ppermute | solution.py:33
  198.0 36.8 %copy-start.3 = (s32[1024]{0:T(1024)S(1)}, s32[1024]{0:T(1024)}, u32[]{:S(2)}) copy-start(s32[1024]{0:T(1024)} %param.5) | copy-start | bytes 12292
  234.7 33.7 %copy-start = (bf16[1024,1024]{1,0:T(8,128)(2,1)S(1)}, bf16[1024,1024]{1,0:T(8,128)(2,1)}, u32[]{:S(2)}) copy-start(bf16[1024,1024]{1,0:T(8,128)(2,1)} %all-gather.5.cloned.1.call-done) | copy-start | bytes 6291460
  235.1 3.2 collective-permute-start.20
  238.3 5.6 %collective-permute-start.21 = (f32[8,384]{1,0:T(8,128)S(1)}, f32[8,384]{1,0:T(8,128)S(1)}, u32[]{:S(2)}, u32[]{:S(2)}) collective-permute-start(f32[8,384]{1,0:T(8,128)S(1)} %fusion.10), channel_id=1, source_target_pairs={{0,32},{16,48},{32,0},{48,16},{64,96},{80,112},{96,64},{112,80},{1... | collective-permute-start | bytes 36872 | tf_op jit(solution)/shard_map/ppermute | solution.py:16
  243.9 7.1 %collective-permute-start.22 = (f32[8,384]{1,0:T(8,128)S(1)}, f32[8,384]{1,0:T(8,128)S(1)}, u32[]{:S(2)}, u32[]{:S(2)}) collective-permute-start(f32[8,384]{1,0:T(8,128)S(1)} %add.185), channel_id=1, source_target_pairs={{0,64},{16,80},{32,96},{48,112},{64,0},{80,16},{96,32},{112,48},{1... | collective-permute-start | bytes 36872 | tf_op jit(solution)/shard_map/ppermute | solution.py:16
  251.0 5.6 %collective-permute-start.23 = (f32[8,384]{1,0:T(8,128)S(1)}, f32[8,384]{1,0:T(8,128)S(1)}, u32[]{:S(2)}, u32[]{:S(2)}) collective-permute-start(f32[8,384]{1,0:T(8,128)S(1)} %add.186), channel_id=1, source_target_pairs={{0,128},{16,144},{32,160},{48,176},{64,192},{80,208},{96,224},{112... | collective-permute-start | bytes 36872 | tf_op jit(solution)/shard_map/ppermute | solution.py:16
  256.6 7.1 %collective-permute-start.24 = (f32[8,384]{1,0:T(8,128)S(1)}, f32[8,384]{1,0:T(8,128)S(1)}, u32[]{:S(2)}, u32[]{:S(2)}) collective-permute-start(f32[8,384]{1,0:T(8,128)S(1)} %add.187), channel_id=1, source_target_pairs={{0,256},{16,272},{32,288},{48,304},{64,320},{80,336},{96,352},{112... | collective-permute-start | bytes 36872 | tf_op jit(solution)/shard_map/ppermute | solution.py:16
  266.5 6.4 %collective-permute-start.10 = (f32[2,2,2,2,32,256]{5,4,2,1,0,3:T(8,128)}, f32[2,2,2,2,32,256]{5,4,2,1,0,3:T(8,128)}, u32[]{:S(2)}, u32[]{:S(2)}) collective-permute-start(f32[2,2,2,2,32,256]{5,4,2,1,0,3:T(8,128)} %bitcast.117), channel_id=1, source_target_pairs={{0,16},{16,0},{32,48},{48,32},{64,80},{80,64},{96,112},{112,96},{1... | collective-permute-start | bytes 1572872 | tf_op jit(solution)/shard_map/ppermute | solution.py:33
  274.0 36.5 %collective-permute-start.11 = (f32[2,2,2,32,256]{4,3,2,1,0:T(8,128)S(1)}, f32[2,2,2,32,256]{4,3,2,1,0:T(8,128)}, u32[]{:S(2)}, u32[]{:S(2)}) collective-permute-start(f32[2,2,2,32,256]{4,3,2,1,0:T(8,128)S(1)} %dynamic-slice_bitcast_fusion.1), channel_id=1, source_target_pairs={{0,32},{16,48},{32,0},{48,16},{64,96},{80,112},{96,64},{112,80},{1... | collective-permute-start | bytes 786440 | tf_op jit(solution)/shard_map/ppermute | solution.py:33
  304.5 2.3 copy-start.1
  307.5 2.3 copy-start.4
  307.8 7.1 %collective-permute-start.15 = (f32[2,2,2,2,40,256]{5,4,2,1,0,3:T(8,128)S(1)}, f32[2,2,2,2,40,256]{5,4,2,1,0,3:T(8,128)S(1)}, u32[]{:S(2)}, u32[]{:S(2)}) collective-permute-start(f32[2,2,2,2,40,256]{5,4,2,1,0,3:T(8,128)S(1)} %bitcast.127), channel_id=1, source_target_pairs={{0,16},{16,0},{32,48},{48,32},{64,80},{80,64},{96,112},{112,96},{1... | collective-permute-start | bytes 1966088 | tf_op jit(solution)/shard_map/ppermute | solution.py:33
  311.5 7.8 %collective-permute-start.12 = (f32[2,2,32,256]{3,2,1,0:T(8,128)S(1)}, f32[2,2,32,256]{3,2,1,0:T(8,128)S(1)}, u32[]{:S(2)}, u32[]{:S(2)}) collective-permute-start(f32[2,2,32,256]{3,2,1,0:T(8,128)S(1)} %dynamic-slice_bitcast_fusion.5), channel_id=1, source_target_pairs={{0,128},{16,144},{32,160},{48,176},{64,192},{80,208},{96,224},{112... | collective-permute-start | bytes 393224 | tf_op jit(solution)/shard_map/ppermute | solution.py:33
  315.0 12.4 %collective-permute-start.16 = (f32[2,2,2,40,256]{4,3,2,1,0:T(8,128)S(1)}, f32[2,2,2,40,256]{4,3,2,1,0:T(8,128)S(1)}, u32[]{:S(2)}, u32[]{:S(2)}) collective-permute-start(f32[2,2,2,40,256]{4,3,2,1,0:T(8,128)S(1)} %dynamic-slice_bitcast_fusion), channel_id=1, source_target_pairs={{0,32},{16,48},{32,0},{48,16},{64,96},{80,112},{96,64},{112,80},{1... | collective-permute-start | bytes 983048 | tf_op jit(solution)/shard_map/ppermute | solution.py:33
  319.3 10.8 %collective-permute-start.13 = (f32[2,32,256]{2,1,0:T(8,128)S(1)}, f32[2,32,256]{2,1,0:T(8,128)S(1)}, u32[]{:S(2)}, u32[]{:S(2)}) collective-permute-start(f32[2,32,256]{2,1,0:T(8,128)S(1)} %dynamic-slice_bitcast_fusion.9), channel_id=1, source_target_pairs={{0,64},{16,80},{32,96},{48,112},{64,0},{80,16},{96,32},{112,48},{1... | collective-permute-start | bytes 196616 | tf_op jit(solution)/shard_map/ppermute | solution.py:33
  327.5 7.2 %collective-permute-start.17 = (f32[2,2,40,256]{3,2,1,0:T(8,128)S(1)}, f32[2,2,40,256]{3,2,1,0:T(8,128)S(1)}, u32[]{:S(2)}, u32[]{:S(2)}) collective-permute-start(f32[2,2,40,256]{3,2,1,0:T(8,128)S(1)} %dynamic-slice_bitcast_fusion.4), channel_id=1, source_target_pairs={{0,128},{16,144},{32,160},{48,176},{64,192},{80,208},{96,224},{112... | collective-permute-start | bytes 491528 | tf_op jit(solution)/shard_map/ppermute | solution.py:33
  334.8 9.6 %collective-permute-start.18 = (f32[2,40,256]{2,1,0:T(8,128)S(1)}, f32[2,40,256]{2,1,0:T(8,128)S(1)}, u32[]{:S(2)}, u32[]{:S(2)}) collective-permute-start(f32[2,40,256]{2,1,0:T(8,128)S(1)} %dynamic-slice_bitcast_fusion.8), channel_id=1, source_target_pairs={{0,64},{16,80},{32,96},{48,112},{64,0},{80,16},{96,32},{112,48},{1... | collective-permute-start | bytes 245768 | tf_op jit(solution)/shard_map/ppermute | solution.py:33
  339.7 7.6 %collective-permute-start.14 = (f32[32,256]{1,0:T(8,128)S(1)}, f32[32,256]{1,0:T(8,128)S(1)}, u32[]{:S(2)}, u32[]{:S(2)}) collective-permute-start(f32[32,256]{1,0:T(8,128)S(1)} %dynamic-slice_bitcast_fusion.13), channel_id=1, source_target_pairs={{0,256},{16,272},{32,288},{48,304},{64,320},{80,336},{96,352},{112... | collective-permute-start | bytes 98312 | tf_op jit(solution)/shard_map/ppermute | solution.py:33
  344.4 7.4 %collective-permute-start.19 = (f32[40,256]{1,0:T(8,128)S(1)}, f32[40,256]{1,0:T(8,128)S(1)}, u32[]{:S(2)}, u32[]{:S(2)}) collective-permute-start(f32[40,256]{1,0:T(8,128)S(1)} %dynamic-slice_bitcast_fusion.12), channel_id=1, source_target_pairs={{0,256},{16,272},{32,288},{48,304},{64,320},{80,336},{96,352},{112... | collective-permute-start | bytes 122888 | tf_op jit(solution)/shard_map/ppermute | solution.py:33
Sparse Core Ops, SparseCore 0:
  10.6 76.6 all-gather.4
  89.8 69.4 all-gather.6
  161.8 69.5 all-gather.8
  234.9 69.6 all-gather.10
where the time goes:
time: 360 us; the launch traced here: 359 us
  waiting for transfers between devices  229 us (64%)
  starting transfers between devices  89.7 us (25%)
  between operations  14.4 us (4%)
  other arithmetic  10.6 us (3%)
  matrix products  8.88 us (2%)
  local copies, waits for them, and re-layouts  6.2 us (2%)
    all_gather x4, waiting for transfers between devices, body(): g = lax.all_gather(part, 'tensor', axis=0, tiled=True)  172 us
    ppermute x20, starting transfers between devices, butterfly_scatter(): x = keep + lax.ppermute(send, axis, perm)  70.9 us
    ppermute x20, waiting for transfers between devices, butterfly_scatter(): x = keep + lax.ppermute(send, axis, perm)  47.8 us
    ppermute x5, starting transfers between devices, butterfly_sum(): x = x + lax.ppermute(x, axis, perm)  18.6 us
    ppermute x5, waiting for transfers between devices, butterfly_sum(): x = x + lax.ppermute(x, axis, perm)  9.86 us
    dot_general x4, matrix products, body(): lax.dot_general(g, activations, (((1,), (0,)), ((), ())), preferred_eleme...  8.7 us
  transfers between devices with their start and end apart: 29, of which 24 were waited for; matrix products, arithmetic and copies ran while one was open for 4% of the time, Pallas kernels for 0%

commit v1 on v0

--- a/solution.py
+++ b/solution.py
@@ -61,7 +61,32 @@
     colsums = []
     for k in range(CHUNKS):
         part = parts[k]
-        g = lax.all_gather(part, "tensor", axis=0, tiled=True)
+
+        def order_quarters(s0):
+            low = lax.axis_size("tensor")
+            upper, state_now, h_now = (low, lax.axis_index("tensor"), s0.shape[0])
+            made = tuple((nth * upper if k0 == 0 else nth for k0, nth in enumerate(s0.shape)))
+            s_next = jnp.zeros(made, s0.dtype)
+            t1 = lax.dynamic_update_slice_in_dim(s_next, s0, state_now * h_now, axis=0)
+            front = step_out = s0
+            h = 1
+            while h < upper // 2 + 1:
+                front = lax.ppermute(
+                    front, "tensor", tuple(((k0, (k0 + 1) % upper) for k0 in range(upper)))
+                )
+                t1 = lax.dynamic_update_slice_in_dim(
+                    t1, front, (state_now - h) % upper * h_now, axis=0
+                )
+                if 2 * h < upper:
+                    outcome_arr = tuple(((k0, (k0 - 1) % upper) for k0 in range(upper)))
+                    step_out = lax.ppermute(step_out, "tensor", outcome_arr)
+                    t1 = lax.dynamic_update_slice_in_dim(
+                        t1, step_out, (state_now + h) % upper * h_now, axis=0
+                    )
+                h += 1
+            return t1
+
+        g = order_quarters(part)
         prod = lax.dot_general(
             g, activations, (((1,), (0,)), ((), ())), preferred_element_type=jnp.float32
         ).reshape(n_dp, w, slice_width)

time: 360 us -> 374 us (1.039)
  the two profiles are of different devices: /device:TPU:32 before, /device:TPU:6 now
where the time goes in v1:
time: 374 us; the launch traced here: 371 us
  starting transfers between devices  297 us (79%)
  waiting for transfers between devices  58.6 us (16%)
  local copies, waits for them, and re-layouts  5.32 us (1%)
  matrix products  4.09 us (1%)
  other arithmetic  3.84 us (1%)
    ppermute x28, starting transfers between devices, order_quarters(): step_out = lax.ppermute(step_out, 'tensor', outcome_arr)  146 us
    ppermute x20, starting transfers between devices, butterfly_scatter(): x = keep + lax.ppermute(send, axis, perm)  68.6 us
    ppermute x32, starting transfers between devices, order_quarters(): lax.ppermute(front, 'tensor', tuple(((k0, (k0 + 1) % upper) for k0 in ran...  61.3 us
    ppermute x32, waiting for transfers between devices, order_quarters(): lax.ppermute(front, 'tensor', tuple(((k0, (k0 + 1) % upper) for k0 in ran...  33 us
    ppermute x5, starting transfers between devices, butterfly_sum(): x = x + lax.ppermute(x, axis, perm)  20.4 us
    ppermute x20, waiting for transfers between devices, butterfly_scatter(): x = keep + lax.ppermute(send, axis, perm)  19.3 us
  transfers between devices with their start and end apart: 85, of which 32 were waited for; matrix products, arithmetic and copies ran while one was open for 2% of the time, Pallas kernels for 0%

profile of v1, /device:TPU:6, one launch (start us, length us, event | category | flops | bytes accessed | tf_op | source)
XLA Modules:
  0.0 371.5 jit_solution(13238996494468286477)
XLA Ops:
  5.8 2.7 collective-permute-start.81
  11.4 7.2 %collective-permute-start.82 = (f32[8,384]{1,0:T(8,128)S(1)}, f32[8,384]{1,0:T(8,128)S(1)}, u32[]{:S(2)}, u32[]{:S(2)}) collective-permute-start(f32[8,384]{1,0:T(8,128)S(1)} %add.460), channel_id=1, source_target_pairs={{0,64},{16,80},{32,96},{48,112},{64,0},{80,16},{96,32},{112,48},{1... | collective-permute-start | bytes 36872 | tf_op jit(solution)/shard_map/ppermute | solution.py:16
  18.6 1.9 collective-permute-start
  20.6 7.5 %collective-permute-start.1 = (bf16[64,1024]{1,0:T(8,128)(2,1)S(1)}, bf16[64,1024]{1,0:T(8,128)(2,1)S(1)}, u32[]{:S(2)}, u32[]{:S(2)}) collective-permute-start(bf16[64,1024]{1,0:T(8,128)(2,1)S(1)} %bitcast.141), channel_id=1, source_target_pairs={{0,15},{1,0},{2,1},{3,2},{4,3},{5,4},{6,5},{7,6},{8,7},{9,8},{10,9... | collective-permute-start | bytes 393224 | tf_op jit(solution)/shard_map/ppermute | solution.py:82
  28.1 3.5 collective-permute-start.83
  33.7 5.1 %collective-permute-start.84 = (f32[8,384]{1,0:T(8,128)S(1)}, f32[8,384]{1,0:T(8,128)S(1)}, u32[]{:S(2)}, u32[]{:S(2)}) collective-permute-start(f32[8,384]{1,0:T(8,128)S(1)} %add.462), channel_id=1, source_target_pairs={{0,256},{16,272},{32,288},{48,304},{64,320},{80,336},{96,352},{112... | collective-permute-start | bytes 36872 | tf_op jit(solution)/shard_map/ppermute | solution.py:16
  40.8 1.9 collective-permute-start.2
  42.8 5.1 %collective-permute-start.3 = (bf16[64,1024]{1,0:T(8,128)(2,1)S(1)}, bf16[64,1024]{1,0:T(8,128)(2,1)S(1)}, u32[]{:S(2)}, u32[]{:S(2)}) collective-permute-start(bf16[64,1024]{1,0:T(8,128)(2,1)S(1)} %collective-permute-done.1), channel_id=1, source_target_pairs={{0,15},{1,0},{2,1},{3,2},{4,3},{5,4},{6,5},{7,6},{8,7},{9,8},{10,9... | collective-permute-start | bytes 393224 | tf_op jit(solution)/shard_map/ppermute | solution.py:82
  50.8 5.1 %collective-permute-start.5 = (bf16[64,1024]{1,0:T(8,128)(2,1)S(1)}, bf16[64,1024]{1,0:T(8,128)(2,1)S(1)}, u32[]{:S(2)}, u32[]{:S(2)}) collective-permute-start(bf16[64,1024]{1,0:T(8,128)(2,1)S(1)} %collective-permute-done.3), channel_id=1, source_target_pairs={{0,15},{1,0},{2,1},{3,2},{4,3},{5,4},{6,5},{7,6},{8,7},{9,8},{10,9... | collective-permute-start | bytes 393224 | tf_op jit(solution)/shard_map/ppermute | solution.py:82
  59.4 5.4 %collective-permute-start.7 = (bf16[64,1024]{1,0:T(8,128)(2,1)S(1)}, bf16[64,1024]{1,0:T(8,128)(2,1)S(1)}, u32[]{:S(2)}, u32[]{:S(2)}) collective-permute-start(bf16[64,1024]{1,0:T(8,128)(2,1)S(1)} %collective-permute-done.5), channel_id=1, source_target_pairs={{0,15},{1,0},{2,1},{3,2},{4,3},{5,4},{6,5},{7,6},{8,7},{9,8},{10,9... | collective-permute-start | bytes 393224 | tf_op jit(solution)/shard_map/ppermute | solution.py:82
  68.6 5.1 %collective-permute-start.9 = (bf16[64,1024]{1,0:T(8,128)(2,1)S(1)}, bf16[64,1024]{1,0:T(8,128)(2,1)S(1)}, u32[]{:S(2)}, u32[]{:S(2)}) collective-permute-start(bf16[64,1024]{1,0:T(8,128)(2,1)S(1)} %collective-permute-done.7), channel_id=1, source_target_pairs={{0,15},{1,0},{2,1},{3,2},{4,3},{5,4},{6,5},{7,6},{8,7},{9,8},{10,9... | collective-permute-start | bytes 393224 | tf_op jit(solution)/shard_map/ppermute | solution.py:82
  77.0 5.1 %collective-permute-start.11 = (bf16[64,1024]{1,0:T(8,128)(2,1)S(1)}, bf16[64,1024]{1,0:T(8,128)(2,1)S(1)}, u32[]{:S(2)}, u32[]{:S(2)}) collective-permute-start(bf16[64,1024]{1,0:T(8,128)(2,1)S(1)} %collective-permute-done.9), channel_id=1, source_target_pairs={{0,15},{1,0},{2,1},{3,2},{4,3},{5,4},{6,5},{7,6},{8,7},{9,8},{10,9... | collective-permute-start | bytes 393224 | tf_op jit(solution)/shard_map/ppermute | solution.py:82
  85.1 5.1 %collective-permute-start.13 = (bf16[64,1024]{1,0:T(8,128)(2,1)S(1)}, bf16[64,1024]{1,0:T(8,128)(2,1)S(1)}, u32[]{:S(2)}, u32[]{:S(2)}) collective-permute-start(bf16[64,1024]{1,0:T(8,128)(2,1)S(1)} %collective-permute-done.11), channel_id=1, source_target_pairs={{0,15},{1,0},{2,1},{3,2},{4,3},{5,4},{6,5},{7,6},{8,7},{9,8},{10,9... | collective-permute-start | bytes 393224 | tf_op jit(solution)/shard_map/ppermute | solution.py:82
  93.2 6.1 %collective-permute-done.14 = bf16[64,1024]{1,0:T(8,128)(2,1)S(1)} collective-permute-done((bf16[64,1024]{1,0:T(8,128)(2,1)S(1)}, bf16[64,1024]{1,0:T(8,128)(2,1)S(1)}, u32[]{:S(2)}, u32[]{:S(2)}) %collective-permute-start.14) | collective-permute-done | bytes 131104 | tf_op jit(solution)/shard_map/ppermute | solution.py:74
  100.0 1.9 collective-permute-start.20
  102.0 5.1 %collective-permute-start.21 = (bf16[64,1024]{1,0:T(8,128)(2,1)S(1)}, bf16[64,1024]{1,0:T(8,128)(2,1)S(1)}, u32[]{:S(2)}, u32[]{:S(2)}) collective-permute-start(bf16[64,1024]{1,0:T(8,128)(2,1)S(1)} %bitcast.138), channel_id=1, source_target_pairs={{0,15},{1,0},{2,1},{3,2},{4,3},{5,4},{6,5},{7,6},{8,7},{9,8},{10,9... | collective-permute-start | bytes 393224 | tf_op jit(solution)/shard_map/ppermute | solution.py:82
  107.6 1.9 collective-permute-start.15
  109.9 1.9 collective-permute-start.22
  111.8 5.1 %collective-permute-start.23 = (bf16[64,1024]{1,0:T(8,128)(2,1)S(1)}, bf16[64,1024]{1,0:T(8,128)(2,1)S(1)}, u32[]{:S(2)}, u32[]{:S(2)}) collective-permute-start(bf16[64,1024]{1,0:T(8,128)(2,1)S(1)} %collective-permute-done.21), channel_id=1, source_target_pairs={{0,15},{1,0},{2,1},{3,2},{4,3},{5,4},{6,5},{7,6},{8,7},{9,8},{10,9... | collective-permute-start | bytes 393224 | tf_op jit(solution)/shard_map/ppermute | solution.py:82
  120.8 5.1 %collective-permute-start.25 = (bf16[64,1024]{1,0:T(8,128)(2,1)S(1)}, bf16[64,1024]{1,0:T(8,128)(2,1)S(1)}, u32[]{:S(2)}, u32[]{:S(2)}) collective-permute-start(bf16[64,1024]{1,0:T(8,128)(2,1)S(1)} %collective-permute-done.23), channel_id=1, source_target_pairs={{0,15},{1,0},{2,1},{3,2},{4,3},{5,4},{6,5},{7,6},{8,7},{9,8},{10,9... | collective-permute-start | bytes 393224 | tf_op jit(solution)/shard_map/ppermute | solution.py:82
  128.9 5.1 %collective-permute-start.27 = (bf16[64,1024]{1,0:T(8,128)(2,1)S(1)}, bf16[64,1024]{1,0:T(8,128)(2,1)S(1)}, u32[]{:S(2)}, u32[]{:S(2)}) collective-permute-start(bf16[64,1024]{1,0:T(8,128)(2,1)S(1)} %collective-permute-done.25), channel_id=1, source_target_pairs={{0,15},{1,0},{2,1},{3,2},{4,3},{5,4},{6,5},{7,6},{8,7},{9,8},{10,9... | collective-permute-start | bytes 393224 | tf_op jit(solution)/shard_map/ppermute | solution.py:82
  137.0 5.1 %collective-permute-start.29 = (bf16[64,1024]{1,0:T(8,128)(2,1)S(1)}, bf16[64,1024]{1,0:T(8,128)(2,1)S(1)}, u32[]{:S(2)}, u32[]{:S(2)}) collective-permute-start(bf16[64,1024]{1,0:T(8,128)(2,1)S(1)} %collective-permute-done.27), channel_id=1, source_target_pairs={{0,15},{1,0},{2,1},{3,2},{4,3},{5,4},{6,5},{7,6},{8,7},{9,8},{10,9... | collective-permute-start | bytes 393224 | tf_op jit(solution)/shard_map/ppermute | solution.py:82
  142.3 1.9 collective-permute-start.16
  146.2 5.1 %collective-permute-start.31 = (bf16[64,1024]{1,0:T(8,128)(2,1)S(1)}, bf16[64,1024]{1,0:T(8,128)(2,1)S(1)}, u32[]{:S(2)}, u32[]{:S(2)}) collective-permute-start(bf16[64,1024]{1,0:T(8,128)(2,1)S(1)} %collective-permute-done.29), channel_id=1, source_target_pairs={{0,15},{1,0},{2,1},{3,2},{4,3},{5,4},{6,5},{7,6},{8,7},{9,8},{10,9... | collective-permute-start | bytes 393224 | tf_op jit(solution)/shard_map/ppermute | solution.py:82
  151.5 3.5 collective-permute-start.17
  156.9 5.1 %collective-permute-start.33 = (bf16[64,1024]{1,0:T(8,128)(2,1)S(1)}, bf16[64,1024]{1,0:T(8,128)(2,1)S(1)}, u32[]{:S(2)}, u32[]{:S(2)}) collective-permute-start(bf16[64,1024]{1,0:T(8,128)(2,1)S(1)} %collective-permute-done.31), channel_id=1, source_target_pairs={{0,15},{1,0},{2,1},{3,2},{4,3},{5,4},{6,5},{7,6},{8,7},{9,8},{10,9... | collective-permute-start | bytes 393224 | tf_op jit(solution)/shard_map/ppermute | solution.py:82
  162.2 5.5 %collective-permute-start.18 = (f32[2,32,256]{2,1,0:T(8,128)S(1)}, f32[2,32,256]{2,1,0:T(8,128)S(1)}, u32[]{:S(2)}, u32[]{:S(2)}) collective-permute-start(f32[2,32,256]{2,1,0:T(8,128)S(1)} %dynamic-slice_bitcast_fusion.11), channel_id=1, source_target_pairs={{0,64},{16,80},{32,96},{48,112},{64,0},{80,16},{96,32},{112,48},{1... | collective-permute-start | bytes 196616 | tf_op jit(solution)/shard_map/ppermute | solution.py:33
  169.9 4.8 %collective-permute-start.19 = (f32[32,256]{1,0:T(8,128)S(1)}, f32[32,256]{1,0:T(8,128)S(1)}, u32[]{:S(2)}, u32[]{:S(2)}) collective-permute-start(f32[32,256]{1,0:T(8,128)S(1)} %dynamic-slice_bitcast_fusion.15), channel_id=1, source_target_pairs={{0,256},{16,272},{32,288},{48,304},{64,320},{80,336},{96,352},{112... | collective-permute-start | bytes 98312 | tf_op jit(solution)/shard_map/ppermute | solution.py:33
  174.7 2.5 collective-permute-done.19
  177.9 1.9 collective-permute-start.40
  179.9 5.1 %collective-permute-start.41 = (bf16[64,1024]{1,0:T(8,128)(2,1)S(1)}, bf16[64,1024]{1,0:T(8,128)(2,1)S(1)}, u32[]{:S(2)}, u32[]{:S(2)}) collective-permute-start(bf16[64,1024]{1,0:T(8,128)(2,1)S(1)} %bitcast.135), channel_id=1, source_target_pairs={{0,15},{1,0},{2,1},{3,2},{4,3},{5,4},{6,5},{7,6},{8,7},{9,8},{10,9... | collective-permute-start | bytes 393224 | tf_op jit(solution)/shard_map/ppermute | solution.py:82
  185.5 1.9 collective-permute-start.35
  187.8 1.9 collective-permute-start.42
  189.8 5.1 %collective-permute-start.43 = (bf16[64,1024]{1,0:T(8,128)(2,1)S(1)}, bf16[64,1024]{1,0:T(8,128)(2,1)S(1)}, u32[]{:S(2)}, u32[]{:S(2)}) collective-permute-start(bf16[64,1024]{1,0:T(8,128)(2,1)S(1)} %collective-permute-done.41), channel_id=1, source_target_pairs={{0,15},{1,0},{2,1},{3,2},{4,3},{5,4},{6,5},{7,6},{8,7},{9,8},{10,9... | collective-permute-start | bytes 393224 | tf_op jit(solution)/shard_map/ppermute | solution.py:82
  198.8 5.1 %collective-permute-start.45 = (bf16[64,1024]{1,0:T(8,128)(2,1)S(1)}, bf16[64,1024]{1,0:T(8,128)(2,1)S(1)}, u32[]{:S(2)}, u32[]{:S(2)}) collective-permute-start(bf16[64,1024]{1,0:T(8,128)(2,1)S(1)} %collective-permute-done.43), channel_id=1, source_target_pairs={{0,15},{1,0},{2,1},{3,2},{4,3},{5,4},{6,5},{7,6},{8,7},{9,8},{10,9... | collective-permute-start | bytes 393224 | tf_op jit(solution)/shard_map/ppermute | solution.py:82
  206.9 5.1 %collective-permute-start.47 = (bf16[64,1024]{1,0:T(8,128)(2,1)S(1)}, bf16[64,1024]{1,0:T(8,128)(2,1)S(1)}, u32[]{:S(2)}, u32[]{:S(2)}) collective-permute-start(bf16[64,1024]{1,0:T(8,128)(2,1)S(1)} %collective-permute-done.45), channel_id=1, source_target_pairs={{0,15},{1,0},{2,1},{3,2},{4,3},{5,4},{6,5},{7,6},{8,7},{9,8},{10,9... | collective-permute-start | bytes 393224 | tf_op jit(solution)/shard_map/ppermute | solution.py:82
  212.2 3.9 %collective-permute-start.36 = (f32[2,2,2,32,256]{4,3,2,1,0:T(8,128)S(1)}, f32[2,2,2,32,256]{4,3,2,1,0:T(8,128)S(1)}, u32[]{:S(2)}, u32[]{:S(2)}) collective-permute-start(f32[2,2,2,32,256]{4,3,2,1,0:T(8,128)S(1)} %dynamic-slice_bitcast_fusion.2), channel_id=1, source_target_pairs={{0,32},{16,48},{32,0},{48,16},{64,96},{80,112},{96,64},{112,80},{1... | collective-permute-start | bytes 786440 | tf_op jit(solution)/shard_map/ppermute | solution.py:33
  218.1 5.1 %collective-permute-start.49 = (bf16[64,1024]{1,0:T(8,128)(2,1)S(1)}, bf16[64,1024]{1,0:T(8,128)(2,1)S(1)}, u32[]{:S(2)}, u32[]{:S(2)}) collective-permute-start(bf16[64,1024]{1,0:T(8,128)(2,1)S(1)} %collective-permute-done.47), channel_id=1, source_target_pairs={{0,15},{1,0},{2,1},{3,2},{4,3},{5,4},{6,5},{7,6},{8,7},{9,8},{10,9... | collective-permute-start | bytes 393224 | tf_op jit(solution)/shard_map/ppermute | solution.py:82
  226.1 5.1 %collective-permute-start.51 = (bf16[64,1024]{1,0:T(8,128)(2,1)S(1)}, bf16[64,1024]{1,0:T(8,128)(2,1)S(1)}, u32[]{:S(2)}, u32[]{:S(2)}) collective-permute-start(bf16[64,1024]{1,0:T(8,128)(2,1)S(1)} %collective-permute-done.49), channel_id=1, source_target_pairs={{0,15},{1,0},{2,1},{3,2},{4,3},{5,4},{6,5},{7,6},{8,7},{9,8},{10,9... | collective-permute-start | bytes 393224 | tf_op jit(solution)/shard_map/ppermute | solution.py:82
  231.4 2.4 collective-permute-start.37
  235.7 5.1 %collective-permute-start.53 = (bf16[64,1024]{1,0:T(8,128)(2,1)S(1)}, bf16[64,1024]{1,0:T(8,128)(2,1)S(1)}, u32[]{:S(2)}, u32[]{:S(2)}) collective-permute-start(bf16[64,1024]{1,0:T(8,128)(2,1)S(1)} %collective-permute-done.51), channel_id=1, source_target_pairs={{0,15},{1,0},{2,1},{3,2},{4,3},{5,4},{6,5},{7,6},{8,7},{9,8},{10,9... | collective-permute-start | bytes 393224 | tf_op jit(solution)/shard_map/ppermute | solution.py:82
  240.9 4.0 %collective-permute-start.38 = (f32[2,32,256]{2,1,0:T(8,128)S(1)}, f32[2,32,256]{2,1,0:T(8,128)S(1)}, u32[]{:S(2)}, u32[]{:S(2)}) collective-permute-start(f32[2,32,256]{2,1,0:T(8,128)S(1)} %dynamic-slice_bitcast_fusion.10), channel_id=1, source_target_pairs={{0,64},{16,80},{32,96},{48,112},{64,0},{80,16},{96,32},{112,48},{1... | collective-permute-start | bytes 196616 | tf_op jit(solution)/shard_map/ppermute | solution.py:33
  245.0 1.9 collective-permute-start.54
  248.6 5.1 %collective-permute-start.39 = (f32[32,256]{1,0:T(8,128)S(1)}, f32[32,256]{1,0:T(8,128)S(1)}, u32[]{:S(2)}, u32[]{:S(2)}) collective-permute-start(f32[32,256]{1,0:T(8,128)S(1)} %dynamic-slice_bitcast_fusion.14), channel_id=1, source_target_pairs={{0,256},{16,272},{32,288},{48,304},{64,320},{80,336},{96,352},{112... | collective-permute-start | bytes 98312 | tf_op jit(solution)/shard_map/ppermute | solution.py:33
  253.8 2.2 collective-permute-done.39
  258.6 5.1 %collective-permute-start.61 = (bf16[64,1024]{1,0:T(8,128)(2,1)S(1)}, bf16[64,1024]{1,0:T(8,128)(2,1)S(1)}, u32[]{:S(2)}, u32[]{:S(2)}) collective-permute-start(bf16[64,1024]{1,0:T(8,128)(2,1)S(1)} %bitcast.132), channel_id=1, source_target_pairs={{0,15},{1,0},{2,1},{3,2},{4,3},{5,4},{6,5},{7,6},{8,7},{9,8},{10,9... | collective-permute-start | bytes 393224 | tf_op jit(solution)/shard_map/ppermute | solution.py:82
  268.5 5.1 %collective-permute-start.63 = (bf16[64,1024]{1,0:T(8,128)(2,1)S(1)}, bf16[64,1024]{1,0:T(8,128)(2,1)S(1)}, u32[]{:S(2)}, u32[]{:S(2)}) collective-permute-start(bf16[64,1024]{1,0:T(8,128)(2,1)S(1)} %collective-permute-done.61), channel_id=1, source_target_pairs={{0,15},{1,0},{2,1},{3,2},{4,3},{5,4},{6,5},{7,6},{8,7},{9,8},{10,9... | collective-permute-start | bytes 393224 | tf_op jit(solution)/shard_map/ppermute | solution.py:82
  277.5 5.1 %collective-permute-start.65 = (bf16[64,1024]{1,0:T(8,128)(2,1)S(1)}, bf16[64,1024]{1,0:T(8,128)(2,1)S(1)}, u32[]{:S(2)}, u32[]{:S(2)}) collective-permute-start(bf16[64,1024]{1,0:T(8,128)(2,1)S(1)} %collective-permute-done.63), channel_id=1, source_target_pairs={{0,15},{1,0},{2,1},{3,2},{4,3},{5,4},{6,5},{7,6},{8,7},{9,8},{10,9... | collective-permute-start | bytes 393224 | tf_op jit(solution)/shard_map/ppermute | solution.py:82
  285.6 5.1 %collective-permute-start.67 = (bf16[64,1024]{1,0:T(8,128)(2,1)S(1)}, bf16[64,1024]{1,0:T(8,128)(2,1)S(1)}, u32[]{:S(2)}, u32[]{:S(2)}) collective-permute-start(bf16[64,1024]{1,0:T(8,128)(2,1)S(1)} %collective-permute-done.65), channel_id=1, source_target_pairs={{0,15},{1,0},{2,1},{3,2},{4,3},{5,4},{6,5},{7,6},{8,7},{9,8},{10,9... | collective-permute-start | bytes 393224 | tf_op jit(solution)/shard_map/ppermute | solution.py:82
  290.9 1.9 collective-permute-start.56
  294.9 5.1 %collective-permute-start.69 = (bf16[64,1024]{1,0:T(8,128)(2,1)S(1)}, bf16[64,1024]{1,0:T(8,128)(2,1)S(1)}, u32[]{:S(2)}, u32[]{:S(2)}) collective-permute-start(bf16[64,1024]{1,0:T(8,128)(2,1)S(1)} %collective-permute-done.67), channel_id=1, source_target_pairs={{0,15},{1,0},{2,1},{3,2},{4,3},{5,4},{6,5},{7,6},{8,7},{9,8},{10,9... | collective-permute-start | bytes 393224 | tf_op jit(solution)/shard_map/ppermute | solution.py:82
  302.9 5.1 %collective-permute-start.71 = (bf16[64,1024]{1,0:T(8,128)(2,1)S(1)}, bf16[64,1024]{1,0:T(8,128)(2,1)S(1)}, u32[]{:S(2)}, u32[]{:S(2)}) collective-permute-start(bf16[64,1024]{1,0:T(8,128)(2,1)S(1)} %collective-permute-done.69), channel_id=1, source_target_pairs={{0,15},{1,0},{2,1},{3,2},{4,3},{5,4},{6,5},{7,6},{8,7},{9,8},{10,9... | collective-permute-start | bytes 393224 | tf_op jit(solution)/shard_map/ppermute | solution.py:82
  311.0 5.1 %collective-permute-start.73 = (bf16[64,1024]{1,0:T(8,128)(2,1)S(1)}, bf16[64,1024]{1,0:T(8,128)(2,1)S(1)}, u32[]{:S(2)}, u32[]{:S(2)}) collective-permute-start(bf16[64,1024]{1,0:T(8,128)(2,1)S(1)} %collective-permute-done.71), channel_id=1, source_target_pairs={{0,15},{1,0},{2,1},{3,2},{4,3},{5,4},{6,5},{7,6},{8,7},{9,8},{10,9... | collective-permute-start | bytes 393224 | tf_op jit(solution)/shard_map/ppermute | solution.py:82
  319.1 6.1 %collective-permute-done.74 = bf16[64,1024]{1,0:T(8,128)(2,1)S(1)} collective-permute-done((bf16[64,1024]{1,0:T(8,128)(2,1)S(1)}, bf16[64,1024]{1,0:T(8,128)(2,1)S(1)}, u32[]{:S(2)}, u32[]{:S(2)}) %collective-permute-start.74) | collective-permute-done | bytes 131104 | tf_op jit(solution)/shard_map/ppermute | solution.py:74
  329.4 3.5 collective-permute-start.57
  333.1 3.9 %collective-permute-start.76 = (f32[2,2,2,40,256]{4,3,2,1,0:T(8,128)S(1)}, f32[2,2,2,40,256]{4,3,2,1,0:T(8,128)S(1)}, u32[]{:S(2)}, u32[]{:S(2)}) collective-permute-start(f32[2,2,2,40,256]{4,3,2,1,0:T(8,128)S(1)} %dynamic-slice_bitcast_fusion), channel_id=1, source_target_pairs={{0,32},{16,48},{32,0},{48,16},{64,96},{80,112},{96,64},{112,80},{1... | collective-permute-start | bytes 983048 | tf_op jit(solution)/shard_map/ppermute | solution.py:33
  337.3 5.4 %collective-permute-start.58 = (f32[2,32,256]{2,1,0:T(8,128)S(1)}, f32[2,32,256]{2,1,0:T(8,128)S(1)}, u32[]{:S(2)}, u32[]{:S(2)}) collective-permute-start(f32[2,32,256]{2,1,0:T(8,128)S(1)} %dynamic-slice_bitcast_fusion.9), channel_id=1, source_target_pairs={{0,64},{16,80},{32,96},{48,112},{64,0},{80,16},{96,32},{112,48},{1... | collective-permute-start | bytes 196616 | tf_op jit(solution)/shard_map/ppermute | solution.py:33
  342.7 2.8 collective-permute-done.76
  345.6 2.4 collective-permute-start.77
  348.3 4.5 %collective-permute-done.77 = f32[2,2,40,256]{3,2,1,0:T(8,128)S(1)} collective-permute-done((f32[2,2,40,256]{3,2,1,0:T(8,128)S(1)}, f32[2,2,40,256]{3,2,1,0:T(8,128)S(1)}, u32[]{:S(2)}, u32[]{:S(2)}) %collective-permute-start.77) | collective-permute-done | bytes 163872 | tf_op jit(solution)/shard_map/ppermute | solution.py:33
  352.9 5.4 %collective-permute-start.78 = (f32[2,40,256]{2,1,0:T(8,128)S(1)}, f32[2,40,256]{2,1,0:T(8,128)S(1)}, u32[]{:S(2)}, u32[]{:S(2)}) collective-permute-start(f32[2,40,256]{2,1,0:T(8,128)S(1)} %dynamic-slice_bitcast_fusion.8), channel_id=1, source_target_pairs={{0,64},{16,80},{32,96},{48,112},{64,0},{80,16},{96,32},{112,48},{1... | collective-permute-start | bytes 245768 | tf_op jit(solution)/shard_map/ppermute | solution.py:33
  358.3 4.8 %collective-permute-start.59 = (f32[32,256]{1,0:T(8,128)S(1)}, f32[32,256]{1,0:T(8,128)S(1)}, u32[]{:S(2)}, u32[]{:S(2)}) collective-permute-start(f32[32,256]{1,0:T(8,128)S(1)} %dynamic-slice_bitcast_fusion.13), channel_id=1, source_target_pairs={{0,256},{16,272},{32,288},{48,304},{64,320},{80,336},{96,352},{112... | collective-permute-start | bytes 98312 | tf_op jit(solution)/shard_map/ppermute | solution.py:33
  363.2 2.5 collective-permute-start.79
  365.7 4.8 %collective-permute-done.79 = f32[40,256]{1,0:T(8,128)S(1)} collective-permute-done((f32[40,256]{1,0:T(8,128)S(1)}, f32[40,256]{1,0:T(8,128)S(1)}, u32[]{:S(2)}, u32[]{:S(2)}) %collective-permute-start.79) | collective-permute-done | bytes 40992 | tf_op jit(solution)/shard_map/ppermute | solution.py:33
  (253 shorter events, 96.4 us)
Async XLA Ops:
  11.4 16.7 %collective-permute-start.82 = (f32[8,384]{1,0:T(8,128)S(1)}, f32[8,384]{1,0:T(8,128)S(1)}, u32[]{:S(2)}, u32[]{:S(2)}) collective-permute-start(f32[8,384]{1,0:T(8,128)S(1)} %add.460), channel_id=1, source_target_pairs={{0,64},{16,80},{32,96},{48,112},{64,0},{80,16},{96,32},{112,48},{1... | collective-permute-start | bytes 36872 | tf_op jit(solution)/shard_map/ppermute | solution.py:16
  18.6 22.2 %collective-permute-start = (bf16[64,1024]{1,0:T(8,128)(2,1)S(1)}, bf16[64,1024]{1,0:T(8,128)(2,1)S(1)}, u32[]{:S(2)}, u32[]{:S(2)}) collective-permute-start(bf16[64,1024]{1,0:T(8,128)(2,1)S(1)} %bitcast.140), channel_id=1, source_target_pairs={{0,1},{1,2},{2,3},{3,4},{4,5},{5,6},{6,7},{7,8},{8,9},{9,10},{10,1... | collective-permute-start | bytes 393224 | tf_op jit(solution)/shard_map/ppermute | solution.py:74
  20.6 22.2 %collective-permute-start.1 = (bf16[64,1024]{1,0:T(8,128)(2,1)S(1)}, bf16[64,1024]{1,0:T(8,128)(2,1)S(1)}, u32[]{:S(2)}, u32[]{:S(2)}) collective-permute-start(bf16[64,1024]{1,0:T(8,128)(2,1)S(1)} %bitcast.141), channel_id=1, source_target_pairs={{0,15},{1,0},{2,1},{3,2},{4,3},{5,4},{6,5},{7,6},{8,7},{9,8},{10,9... | collective-permute-start | bytes 393224 | tf_op jit(solution)/shard_map/ppermute | solution.py:82
  40.8 8.1 %collective-permute-start.2 = (bf16[64,1024]{1,0:T(8,128)(2,1)S(1)}, bf16[64,1024]{1,0:T(8,128)(2,1)S(1)}, u32[]{:S(2)}, u32[]{:S(2)}) collective-permute-start(bf16[64,1024]{1,0:T(8,128)(2,1)S(1)} %collective-permute-done), channel_id=1, source_target_pairs={{0,1},{1,2},{2,3},{3,4},{4,5},{5,6},{6,7},{7,8},{8,9},{9,10},{10,1... | collective-permute-start | bytes 393224 | tf_op jit(solution)/shard_map/ppermute | solution.py:74
  48.9 8.5 %collective-permute-start.4 = (bf16[64,1024]{1,0:T(8,128)(2,1)S(1)}, bf16[64,1024]{1,0:T(8,128)(2,1)S(1)}, u32[]{:S(2)}, u32[]{:S(2)}) collective-permute-start(bf16[64,1024]{1,0:T(8,128)(2,1)S(1)} %collective-permute-done.2), channel_id=1, source_target_pairs={{0,1},{1,2},{2,3},{3,4},{4,5},{5,6},{6,7},{7,8},{8,9},{9,10},{10,1... | collective-permute-start | bytes 393224 | tf_op jit(solution)/shard_map/ppermute | solution.py:74
  50.8 8.5 %collective-permute-start.5 = (bf16[64,1024]{1,0:T(8,128)(2,1)S(1)}, bf16[64,1024]{1,0:T(8,128)(2,1)S(1)}, u32[]{:S(2)}, u32[]{:S(2)}) collective-permute-start(bf16[64,1024]{1,0:T(8,128)(2,1)S(1)} %collective-permute-done.3), channel_id=1, source_target_pairs={{0,15},{1,0},{2,1},{3,2},{4,3},{5,4},{6,5},{7,6},{8,7},{9,8},{10,9... | collective-permute-start | bytes 393224 | tf_op jit(solution)/shard_map/ppermute | solution.py:82
  57.4 9.3 %collective-permute-start.6 = (bf16[64,1024]{1,0:T(8,128)(2,1)S(1)}, bf16[64,1024]{1,0:T(8,128)(2,1)S(1)}, u32[]{:S(2)}, u32[]{:S(2)}) collective-permute-start(bf16[64,1024]{1,0:T(8,128)(2,1)S(1)} %collective-permute-done.4), channel_id=1, source_target_pairs={{0,1},{1,2},{2,3},{3,4},{4,5},{5,6},{6,7},{7,8},{8,9},{9,10},{10,1... | collective-permute-start | bytes 393224 | tf_op jit(solution)/shard_map/ppermute | solution.py:74
  59.4 9.3 %collective-permute-start.7 = (bf16[64,1024]{1,0:T(8,128)(2,1)S(1)}, bf16[64,1024]{1,0:T(8,128)(2,1)S(1)}, u32[]{:S(2)}, u32[]{:S(2)}) collective-permute-start(bf16[64,1024]{1,0:T(8,128)(2,1)S(1)} %collective-permute-done.5), channel_id=1, source_target_pairs={{0,15},{1,0},{2,1},{3,2},{4,3},{5,4},{6,5},{7,6},{8,7},{9,8},{10,9... | collective-permute-start | bytes 393224 | tf_op jit(solution)/shard_map/ppermute | solution.py:82
  66.7 8.4 %collective-permute-start.8 = (bf16[64,1024]{1,0:T(8,128)(2,1)S(1)}, bf16[64,1024]{1,0:T(8,128)(2,1)S(1)}, u32[]{:S(2)}, u32[]{:S(2)}) collective-permute-start(bf16[64,1024]{1,0:T(8,128)(2,1)S(1)} %collective-permute-done.6), channel_id=1, source_target_pairs={{0,1},{1,2},{2,3},{3,4},{4,5},{5,6},{6,7},{7,8},{8,9},{9,10},{10,1... | collective-permute-start | bytes 393224 | tf_op jit(solution)/shard_map/ppermute | solution.py:74
  68.6 8.4 %collective-permute-start.9 = (bf16[64,1024]{1,0:T(8,128)(2,1)S(1)}, bf16[64,1024]{1,0:T(8,128)(2,1)S(1)}, u32[]{:S(2)}, u32[]{:S(2)}) collective-permute-start(bf16[64,1024]{1,0:T(8,128)(2,1)S(1)} %collective-permute-done.7), channel_id=1, source_target_pairs={{0,15},{1,0},{2,1},{3,2},{4,3},{5,4},{6,5},{7,6},{8,7},{9,8},{10,9... | collective-permute-start | bytes 393224 | tf_op jit(solution)/shard_map/ppermute | solution.py:82
  75.1 8.1 %collective-permute-start.10 = (bf16[64,1024]{1,0:T(8,128)(2,1)S(1)}, bf16[64,1024]{1,0:T(8,128)(2,1)S(1)}, u32[]{:S(2)}, u32[]{:S(2)}) collective-permute-start(bf16[64,1024]{1,0:T(8,128)(2,1)S(1)} %collective-permute-done.8), channel_id=1, source_target_pairs={{0,1},{1,2},{2,3},{3,4},{4,5},{5,6},{6,7},{7,8},{8,9},{9,10},{10,1... | collective-permute-start | bytes 393224 | tf_op jit(solution)/shard_map/ppermute | solution.py:74
  83.2 8.1 %collective-permute-start.12 = (bf16[64,1024]{1,0:T(8,128)(2,1)S(1)}, bf16[64,1024]{1,0:T(8,128)(2,1)S(1)}, u32[]{:S(2)}, u32[]{:S(2)}) collective-permute-start(bf16[64,1024]{1,0:T(8,128)(2,1)S(1)} %collective-permute-done.10), channel_id=1, source_target_pairs={{0,1},{1,2},{2,3},{3,4},{4,5},{5,6},{6,7},{7,8},{8,9},{9,10},{10,1... | collective-permute-start | bytes 393224 | tf_op jit(solution)/shard_map/ppermute | solution.py:74
  85.1 8.1 %collective-permute-start.13 = (bf16[64,1024]{1,0:T(8,128)(2,1)S(1)}, bf16[64,1024]{1,0:T(8,128)(2,1)S(1)}, u32[]{:S(2)}, u32[]{:S(2)}) collective-permute-start(bf16[64,1024]{1,0:T(8,128)(2,1)S(1)} %collective-permute-done.11), channel_id=1, source_target_pairs={{0,15},{1,0},{2,1},{3,2},{4,3},{5,4},{6,5},{7,6},{8,7},{9,8},{10,9... | collective-permute-start | bytes 393224 | tf_op jit(solution)/shard_map/ppermute | solution.py:82
  91.2 8.1 %collective-permute-start.14 = (bf16[64,1024]{1,0:T(8,128)(2,1)S(1)}, bf16[64,1024]{1,0:T(8,128)(2,1)S(1)}, u32[]{:S(2)}, u32[]{:S(2)}) collective-permute-start(bf16[64,1024]{1,0:T(8,128)(2,1)S(1)} %collective-permute-done.12), channel_id=1, source_target_pairs={{0,1},{1,2},{2,3},{3,4},{4,5},{5,6},{6,7},{7,8},{8,9},{9,10},{10,1... | collective-permute-start | bytes 393224 | tf_op jit(solution)/shard_map/ppermute | solution.py:74
  100.0 9.8 %collective-permute-start.20 = (bf16[64,1024]{1,0:T(8,128)(2,1)S(1)}, bf16[64,1024]{1,0:T(8,128)(2,1)S(1)}, u32[]{:S(2)}, u32[]{:S(2)}) collective-permute-start(bf16[64,1024]{1,0:T(8,128)(2,1)S(1)} %bitcast.137), channel_id=1, source_target_pairs={{0,1},{1,2},{2,3},{3,4},{4,5},{5,6},{6,7},{7,8},{8,9},{9,10},{10,1... | collective-permute-start | bytes 393224 | tf_op jit(solution)/shard_map/ppermute | solution.py:74
  102.0 9.8 %collective-permute-start.21 = (bf16[64,1024]{1,0:T(8,128)(2,1)S(1)}, bf16[64,1024]{1,0:T(8,128)(2,1)S(1)}, u32[]{:S(2)}, u32[]{:S(2)}) collective-permute-start(bf16[64,1024]{1,0:T(8,128)(2,1)S(1)} %bitcast.138), channel_id=1, source_target_pairs={{0,15},{1,0},{2,1},{3,2},{4,3},{5,4},{6,5},{7,6},{8,7},{9,8},{10,9... | collective-permute-start | bytes 393224 | tf_op jit(solution)/shard_map/ppermute | solution.py:82
  107.6 34.6 %collective-permute-start.15 = (f32[2,2,2,2,32,256]{5,4,2,1,0,3:T(8,128)S(1)}, f32[2,2,2,2,32,256]{5,4,2,1,0,3:T(8,128)S(1)}, u32[]{:S(2)}, u32[]{:S(2)}) collective-permute-start(f32[2,2,2,2,32,256]{5,4,2,1,0,3:T(8,128)S(1)} %bitcast.128), channel_id=1, source_target_pairs={{0,16},{16,0},{32,48},{48,32},{64,80},{80,64},{96,112},{112,96},{1... | collective-permute-start | bytes 1572872 | tf_op jit(solution)/shard_map/ppermute | solution.py:33
  109.9 9.0 %collective-permute-start.22 = (bf16[64,1024]{1,0:T(8,128)(2,1)S(1)}, bf16[64,1024]{1,0:T(8,128)(2,1)S(1)}, u32[]{:S(2)}, u32[]{:S(2)}) collective-permute-start(bf16[64,1024]{1,0:T(8,128)(2,1)S(1)} %collective-permute-done.20), channel_id=1, source_target_pairs={{0,1},{1,2},{2,3},{3,4},{4,5},{5,6},{6,7},{7,8},{8,9},{9,10},{10,1... | collective-permute-start | bytes 393224 | tf_op jit(solution)/shard_map/ppermute | solution.py:74
  111.8 9.0 %collective-permute-start.23 = (bf16[64,1024]{1,0:T(8,128)(2,1)S(1)}, bf16[64,1024]{1,0:T(8,128)(2,1)S(1)}, u32[]{:S(2)}, u32[]{:S(2)}) collective-permute-start(bf16[64,1024]{1,0:T(8,128)(2,1)S(1)} %collective-permute-done.21), channel_id=1, source_target_pairs={{0,15},{1,0},{2,1},{3,2},{4,3},{5,4},{6,5},{7,6},{8,7},{9,8},{10,9... | collective-permute-start | bytes 393224 | tf_op jit(solution)/shard_map/ppermute | solution.py:82
  118.9 8.1 %collective-permute-start.24 = (bf16[64,1024]{1,0:T(8,128)(2,1)S(1)}, bf16[64,1024]{1,0:T(8,128)(2,1)S(1)}, u32[]{:S(2)}, u32[]{:S(2)}) collective-permute-start(bf16[64,1024]{1,0:T(8,128)(2,1)S(1)} %collective-permute-done.22), channel_id=1, source_target_pairs={{0,1},{1,2},{2,3},{3,4},{4,5},{5,6},{6,7},{7,8},{8,9},{9,10},{10,1... | collective-permute-start | bytes 393224 | tf_op jit(solution)/shard_map/ppermute | solution.py:74
  120.8 8.1 %collective-permute-start.25 = (bf16[64,1024]{1,0:T(8,128)(2,1)S(1)}, bf16[64,1024]{1,0:T(8,128)(2,1)S(1)}, u32[]{:S(2)}, u32[]{:S(2)}) collective-permute-start(bf16[64,1024]{1,0:T(8,128)(2,1)S(1)} %collective-permute-done.23), channel_id=1, source_target_pairs={{0,15},{1,0},{2,1},{3,2},{4,3},{5,4},{6,5},{7,6},{8,7},{9,8},{10,9... | collective-permute-start | bytes 393224 | tf_op jit(solution)/shard_map/ppermute | solution.py:82
  127.0 8.1 %collective-permute-start.26 = (bf16[64,1024]{1,0:T(8,128)(2,1)S(1)}, bf16[64,1024]{1,0:T(8,128)(2,1)S(1)}, u32[]{:S(2)}, u32[]{:S(2)}) collective-permute-start(bf16[64,1024]{1,0:T(8,128)(2,1)S(1)} %collective-permute-done.24), channel_id=1, source_target_pairs={{0,1},{1,2},{2,3},{3,4},{4,5},{5,6},{6,7},{7,8},{8,9},{9,10},{10,1... | collective-permute-start | bytes 393224 | tf_op jit(solution)/shard_map/ppermute | solution.py:74
  135.1 9.2 %collective-permute-start.28 = (bf16[64,1024]{1,0:T(8,128)(2,1)S(1)}, bf16[64,1024]{1,0:T(8,128)(2,1)S(1)}, u32[]{:S(2)}, u32[]{:S(2)}) collective-permute-start(bf16[64,1024]{1,0:T(8,128)(2,1)S(1)} %collective-permute-done.26), channel_id=1, source_target_pairs={{0,1},{1,2},{2,3},{3,4},{4,5},{5,6},{6,7},{7,8},{8,9},{9,10},{10,1... | collective-permute-start | bytes 393224 | tf_op jit(solution)/shard_map/ppermute | solution.py:74
  137.0 9.2 %collective-permute-start.29 = (bf16[64,1024]{1,0:T(8,128)(2,1)S(1)}, bf16[64,1024]{1,0:T(8,128)(2,1)S(1)}, u32[]{:S(2)}, u32[]{:S(2)}) collective-permute-start(bf16[64,1024]{1,0:T(8,128)(2,1)S(1)} %collective-permute-done.27), channel_id=1, source_target_pairs={{0,15},{1,0},{2,1},{3,2},{4,3},{5,4},{6,5},{7,6},{8,7},{9,8},{10,9... | collective-permute-start | bytes 393224 | tf_op jit(solution)/shard_map/ppermute | solution.py:82
  142.3 9.1 %collective-permute-start.16 = (f32[2,2,2,32,256]{4,3,2,1,0:T(8,128)S(1)}, f32[2,2,2,32,256]{4,3,2,1,0:T(8,128)S(1)}, u32[]{:S(2)}, u32[]{:S(2)}) collective-permute-start(f32[2,2,2,32,256]{4,3,2,1,0:T(8,128)S(1)} %dynamic-slice_bitcast_fusion.3), channel_id=1, source_target_pairs={{0,32},{16,48},{32,0},{48,16},{64,96},{80,112},{96,64},{112,80},{1... | collective-permute-start | bytes 786440 | tf_op jit(solution)/shard_map/ppermute | solution.py:33
  144.2 10.7 %collective-permute-start.30 = (bf16[64,1024]{1,0:T(8,128)(2,1)S(1)}, bf16[64,1024]{1,0:T(8,128)(2,1)S(1)}, u32[]{:S(2)}, u32[]{:S(2)}) collective-permute-start(bf16[64,1024]{1,0:T(8,128)(2,1)S(1)} %collective-permute-done.28), channel_id=1, source_target_pairs={{0,1},{1,2},{2,3},{3,4},{4,5},{5,6},{6,7},{7,8},{8,9},{9,10},{10,1... | collective-permute-start | bytes 393224 | tf_op jit(solution)/shard_map/ppermute | solution.py:74
  146.2 10.7 %collective-permute-start.31 = (bf16[64,1024]{1,0:T(8,128)(2,1)S(1)}, bf16[64,1024]{1,0:T(8,128)(2,1)S(1)}, u32[]{:S(2)}, u32[]{:S(2)}) collective-permute-start(bf16[64,1024]{1,0:T(8,128)(2,1)S(1)} %collective-permute-done.29), channel_id=1, source_target_pairs={{0,15},{1,0},{2,1},{3,2},{4,3},{5,4},{6,5},{7,6},{8,7},{9,8},{10,9... | collective-permute-start | bytes 393224 | tf_op jit(solution)/shard_map/ppermute | solution.py:82
  151.5 10.6 %collective-permute-start.17 = (f32[2,2,32,256]{3,2,1,0:T(8,128)S(1)}, f32[2,2,32,256]{3,2,1,0:T(8,128)S(1)}, u32[]{:S(2)}, u32[]{:S(2)}) collective-permute-start(f32[2,2,32,256]{3,2,1,0:T(8,128)S(1)} %dynamic-slice_bitcast_fusion.7), channel_id=1, source_target_pairs={{0,128},{16,144},{32,160},{48,176},{64,192},{80,208},{96,224},{112... | collective-permute-start | bytes 393224 | tf_op jit(solution)/shard_map/ppermute | solution.py:33
  155.0 12.7 %collective-permute-start.32 = (bf16[64,1024]{1,0:T(8,128)(2,1)S(1)}, bf16[64,1024]{1,0:T(8,128)(2,1)S(1)}, u32[]{:S(2)}, u32[]{:S(2)}) collective-permute-start(bf16[64,1024]{1,0:T(8,128)(2,1)S(1)} %collective-permute-done.30), channel_id=1, source_target_pairs={{0,1},{1,2},{2,3},{3,4},{4,5},{5,6},{6,7},{7,8},{8,9},{9,10},{10,1... | collective-permute-start | bytes 393224 | tf_op jit(solution)/shard_map/ppermute | solution.py:74
  156.9 17.8 %collective-permute-start.33 = (bf16[64,1024]{1,0:T(8,128)(2,1)S(1)}, bf16[64,1024]{1,0:T(8,128)(2,1)S(1)}, u32[]{:S(2)}, u32[]{:S(2)}) collective-permute-start(bf16[64,1024]{1,0:T(8,128)(2,1)S(1)} %collective-permute-done.31), channel_id=1, source_target_pairs={{0,15},{1,0},{2,1},{3,2},{4,3},{5,4},{6,5},{7,6},{8,7},{9,8},{10,9... | collective-permute-start | bytes 393224 | tf_op jit(solution)/shard_map/ppermute | solution.py:82
  167.6 9.6 %collective-permute-start.34 = (bf16[64,1024]{1,0:T(8,128)(2,1)S(1)}, bf16[64,1024]{1,0:T(8,128)(2,1)S(1)}, u32[]{:S(2)}, u32[]{:S(2)}) collective-permute-start(bf16[64,1024]{1,0:T(8,128)(2,1)S(1)} %collective-permute-done.32), channel_id=1, source_target_pairs={{0,1},{1,2},{2,3},{3,4},{4,5},{5,6},{6,7},{7,8},{8,9},{9,10},{10,1... | collective-permute-start | bytes 393224 | tf_op jit(solution)/shard_map/ppermute | solution.py:74
  177.9 9.9 %collective-permute-start.40 = (bf16[64,1024]{1,0:T(8,128)(2,1)S(1)}, bf16[64,1024]{1,0:T(8,128)(2,1)S(1)}, u32[]{:S(2)}, u32[]{:S(2)}) collective-permute-start(bf16[64,1024]{1,0:T(8,128)(2,1)S(1)} %bitcast.134), channel_id=1, source_target_pairs={{0,1},{1,2},{2,3},{3,4},{4,5},{5,6},{6,7},{7,8},{8,9},{9,10},{10,1... | collective-permute-start | bytes 393224 | tf_op jit(solution)/shard_map/ppermute | solution.py:74
  179.9 9.9 %collective-permute-start.41 = (bf16[64,1024]{1,0:T(8,128)(2,1)S(1)}, bf16[64,1024]{1,0:T(8,128)(2,1)S(1)}, u32[]{:S(2)}, u32[]{:S(2)}) collective-permute-start(bf16[64,1024]{1,0:T(8,128)(2,1)S(1)} %bitcast.135), channel_id=1, source_target_pairs={{0,15},{1,0},{2,1},{3,2},{4,3},{5,4},{6,5},{7,6},{8,7},{9,8},{10,9... | collective-permute-start | bytes 393224 | tf_op jit(solution)/shard_map/ppermute | solution.py:82
  185.5 26.6 %collective-permute-start.35 = (f32[2,2,2,2,32,256]{5,4,2,1,0,3:T(8,128)S(1)}, f32[2,2,2,2,32,256]{5,4,2,1,0,3:T(8,128)S(1)}, u32[]{:S(2)}, u32[]{:S(2)}) collective-permute-start(f32[2,2,2,2,32,256]{5,4,2,1,0,3:T(8,128)S(1)} %bitcast.130), channel_id=1, source_target_pairs={{0,16},{16,0},{32,48},{48,32},{64,80},{80,64},{96,112},{112,96},{1... | collective-permute-start | bytes 1572872 | tf_op jit(solution)/shard_map/ppermute | solution.py:33
  187.8 9.0 %collective-permute-start.42 = (bf16[64,1024]{1,0:T(8,128)(2,1)S(1)}, bf16[64,1024]{1,0:T(8,128)(2,1)S(1)}, u32[]{:S(2)}, u32[]{:S(2)}) collective-permute-start(bf16[64,1024]{1,0:T(8,128)(2,1)S(1)} %collective-permute-done.40), channel_id=1, source_target_pairs={{0,1},{1,2},{2,3},{3,4},{4,5},{5,6},{6,7},{7,8},{8,9},{9,10},{10,1... | collective-permute-start | bytes 393224 | tf_op jit(solution)/shard_map/ppermute | solution.py:74
  189.8 9.0 %collective-permute-start.43 = (bf16[64,1024]{1,0:T(8,128)(2,1)S(1)}, bf16[64,1024]{1,0:T(8,128)(2,1)S(1)}, u32[]{:S(2)}, u32[]{:S(2)}) collective-permute-start(bf16[64,1024]{1,0:T(8,128)(2,1)S(1)} %collective-permute-done.41), channel_id=1, source_target_pairs={{0,15},{1,0},{2,1},{3,2},{4,3},{5,4},{6,5},{7,6},{8,7},{9,8},{10,9... | collective-permute-start | bytes 393224 | tf_op jit(solution)/shard_map/ppermute | solution.py:82
  196.8 8.1 %collective-permute-start.44 = (bf16[64,1024]{1,0:T(8,128)(2,1)S(1)}, bf16[64,1024]{1,0:T(8,128)(2,1)S(1)}, u32[]{:S(2)}, u32[]{:S(2)}) collective-permute-start(bf16[64,1024]{1,0:T(8,128)(2,1)S(1)} %collective-permute-done.42), channel_id=1, source_target_pairs={{0,1},{1,2},{2,3},{3,4},{4,5},{5,6},{6,7},{7,8},{8,9},{9,10},{10,1... | collective-permute-start | bytes 393224 | tf_op jit(solution)/shard_map/ppermute | solution.py:74
  198.8 8.1 %collective-permute-start.45 = (bf16[64,1024]{1,0:T(8,128)(2,1)S(1)}, bf16[64,1024]{1,0:T(8,128)(2,1)S(1)}, u32[]{:S(2)}, u32[]{:S(2)}) collective-permute-start(bf16[64,1024]{1,0:T(8,128)(2,1)S(1)} %collective-permute-done.43), channel_id=1, source_target_pairs={{0,15},{1,0},{2,1},{3,2},{4,3},{5,4},{6,5},{7,6},{8,7},{9,8},{10,9... | collective-permute-start | bytes 393224 | tf_op jit(solution)/shard_map/ppermute | solution.py:82
  205.0 11.1 %collective-permute-start.46 = (bf16[64,1024]{1,0:T(8,128)(2,1)S(1)}, bf16[64,1024]{1,0:T(8,128)(2,1)S(1)}, u32[]{:S(2)}, u32[]{:S(2)}) collective-permute-start(bf16[64,1024]{1,0:T(8,128)(2,1)S(1)} %collective-permute-done.44), channel_id=1, source_target_pairs={{0,1},{1,2},{2,3},{3,4},{4,5},{5,6},{6,7},{7,8},{8,9},{9,10},{10,1... | collective-permute-start | bytes 393224 | tf_op jit(solution)/shard_map/ppermute | solution.py:74
  206.9 11.2 %collective-permute-start.47 = (bf16[64,1024]{1,0:T(8,128)(2,1)S(1)}, bf16[64,1024]{1,0:T(8,128)(2,1)S(1)}, u32[]{:S(2)}, u32[]{:S(2)}) collective-permute-start(bf16[64,1024]{1,0:T(8,128)(2,1)S(1)} %collective-permute-done.45), channel_id=1, source_target_pairs={{0,15},{1,0},{2,1},{3,2},{4,3},{5,4},{6,5},{7,6},{8,7},{9,8},{10,9... | collective-permute-start | bytes 393224 | tf_op jit(solution)/shard_map/ppermute | solution.py:82
  212.2 19.1 %collective-permute-start.36 = (f32[2,2,2,32,256]{4,3,2,1,0:T(8,128)S(1)}, f32[2,2,2,32,256]{4,3,2,1,0:T(8,128)S(1)}, u32[]{:S(2)}, u32[]{:S(2)}) collective-permute-start(f32[2,2,2,32,256]{4,3,2,1,0:T(8,128)S(1)} %dynamic-slice_bitcast_fusion.2), channel_id=1, source_target_pairs={{0,32},{16,48},{32,0},{48,16},{64,96},{80,112},{96,64},{112,80},{1... | collective-permute-start | bytes 786440 | tf_op jit(solution)/shard_map/ppermute | solution.py:33
  216.1 8.1 %collective-permute-start.48 = (bf16[64,1024]{1,0:T(8,128)(2,1)S(1)}, bf16[64,1024]{1,0:T(8,128)(2,1)S(1)}, u32[]{:S(2)}, u32[]{:S(2)}) collective-permute-start(bf16[64,1024]{1,0:T(8,128)(2,1)S(1)} %collective-permute-done.46), channel_id=1, source_target_pairs={{0,1},{1,2},{2,3},{3,4},{4,5},{5,6},{6,7},{7,8},{8,9},{9,10},{10,1... | collective-permute-start | bytes 393224 | tf_op jit(solution)/shard_map/ppermute | solution.py:74
  224.2 9.6 %collective-permute-start.50 = (bf16[64,1024]{1,0:T(8,128)(2,1)S(1)}, bf16[64,1024]{1,0:T(8,128)(2,1)S(1)}, u32[]{:S(2)}, u32[]{:S(2)}) collective-permute-start(bf16[64,1024]{1,0:T(8,128)(2,1)S(1)} %collective-permute-done.48), channel_id=1, source_target_pairs={{0,1},{1,2},{2,3},{3,4},{4,5},{5,6},{6,7},{7,8},{8,9},{9,10},{10,1... | collective-permute-start | bytes 393224 | tf_op jit(solution)/shard_map/ppermute | solution.py:74
  226.1 9.6 %collective-permute-start.51 = (bf16[64,1024]{1,0:T(8,128)(2,1)S(1)}, bf16[64,1024]{1,0:T(8,128)(2,1)S(1)}, u32[]{:S(2)}, u32[]{:S(2)}) collective-permute-start(bf16[64,1024]{1,0:T(8,128)(2,1)S(1)} %collective-permute-done.49), channel_id=1, source_target_pairs={{0,15},{1,0},{2,1},{3,2},{4,3},{5,4},{6,5},{7,6},{8,7},{9,8},{10,9... | collective-permute-start | bytes 393224 | tf_op jit(solution)/shard_map/ppermute | solution.py:82
  231.4 9.5 %collective-permute-start.37 = (f32[2,2,32,256]{3,2,1,0:T(8,128)S(1)}, f32[2,2,32,256]{3,2,1,0:T(8,128)S(1)}, u32[]{:S(2)}, u32[]{:S(2)}) collective-permute-start(f32[2,2,32,256]{3,2,1,0:T(8,128)S(1)} %dynamic-slice_bitcast_fusion.6), channel_id=1, source_target_pairs={{0,128},{16,144},{32,160},{48,176},{64,192},{80,208},{96,224},{112... | collective-permute-start | bytes 393224 | tf_op jit(solution)/shard_map/ppermute | solution.py:33
  233.8 11.2 %collective-permute-start.52 = (bf16[64,1024]{1,0:T(8,128)(2,1)S(1)}, bf16[64,1024]{1,0:T(8,128)(2,1)S(1)}, u32[]{:S(2)}, u32[]{:S(2)}) collective-permute-start(bf16[64,1024]{1,0:T(8,128)(2,1)S(1)} %collective-permute-done.50), channel_id=1, source_target_pairs={{0,1},{1,2},{2,3},{3,4},{4,5},{5,6},{6,7},{7,8},{8,9},{9,10},{10,1... | collective-permute-start | bytes 393224 | tf_op jit(solution)/shard_map/ppermute | solution.py:74
  235.7 18.0 %collective-permute-start.53 = (bf16[64,1024]{1,0:T(8,128)(2,1)S(1)}, bf16[64,1024]{1,0:T(8,128)(2,1)S(1)}, u32[]{:S(2)}, u32[]{:S(2)}) collective-permute-start(bf16[64,1024]{1,0:T(8,128)(2,1)S(1)} %collective-permute-done.51), channel_id=1, source_target_pairs={{0,15},{1,0},{2,1},{3,2},{4,3},{5,4},{6,5},{7,6},{8,7},{9,8},{10,9... | collective-permute-start | bytes 393224 | tf_op jit(solution)/shard_map/ppermute | solution.py:82
  245.0 11.0 %collective-permute-start.54 = (bf16[64,1024]{1,0:T(8,128)(2,1)S(1)}, bf16[64,1024]{1,0:T(8,128)(2,1)S(1)}, u32[]{:S(2)}, u32[]{:S(2)}) collective-permute-start(bf16[64,1024]{1,0:T(8,128)(2,1)S(1)} %collective-permute-done.52), channel_id=1, source_target_pairs={{0,1},{1,2},{2,3},{3,4},{4,5},{5,6},{6,7},{7,8},{8,9},{9,10},{10,1... | collective-permute-start | bytes 393224 | tf_op jit(solution)/shard_map/ppermute | solution.py:74
  256.7 9.8 %collective-permute-start.60 = (bf16[64,1024]{1,0:T(8,128)(2,1)S(1)}, bf16[64,1024]{1,0:T(8,128)(2,1)S(1)}, u32[]{:S(2)}, u32[]{:S(2)}) collective-permute-start(bf16[64,1024]{1,0:T(8,128)(2,1)S(1)} %bitcast.131), channel_id=1, source_target_pairs={{0,1},{1,2},{2,3},{3,4},{4,5},{5,6},{6,7},{7,8},{8,9},{9,10},{10,1... | collective-permute-start | bytes 393224 | tf_op jit(solution)/shard_map/ppermute | solution.py:74
  258.6 9.8 %collective-permute-start.61 = (bf16[64,1024]{1,0:T(8,128)(2,1)S(1)}, bf16[64,1024]{1,0:T(8,128)(2,1)S(1)}, u32[]{:S(2)}, u32[]{:S(2)}) collective-permute-start(bf16[64,1024]{1,0:T(8,128)(2,1)S(1)} %bitcast.132), channel_id=1, source_target_pairs={{0,15},{1,0},{2,1},{3,2},{4,3},{5,4},{6,5},{7,6},{8,7},{9,8},{10,9... | collective-permute-start | bytes 393224 | tf_op jit(solution)/shard_map/ppermute | solution.py:82
  264.3 26.6 %collective-permute-start.55 = (f32[2,2,2,2,32,256]{5,4,2,1,0,3:T(8,128)S(1)}, f32[2,2,2,2,32,256]{5,4,2,1,0,3:T(8,128)S(1)}, u32[]{:S(2)}, u32[]{:S(2)}) collective-permute-start(f32[2,2,2,2,32,256]{5,4,2,1,0,3:T(8,128)S(1)} %bitcast.129), channel_id=1, source_target_pairs={{0,16},{16,0},{32,48},{48,32},{64,80},{80,64},{96,112},{112,96},{1... | collective-permute-start | bytes 1572872 | tf_op jit(solution)/shard_map/ppermute | solution.py:33
  266.6 9.0 %collective-permute-start.62 = (bf16[64,1024]{1,0:T(8,128)(2,1)S(1)}, bf16[64,1024]{1,0:T(8,128)(2,1)S(1)}, u32[]{:S(2)}, u32[]{:S(2)}) collective-permute-start(bf16[64,1024]{1,0:T(8,128)(2,1)S(1)} %collective-permute-done.60), channel_id=1, source_target_pairs={{0,1},{1,2},{2,3},{3,4},{4,5},{5,6},{6,7},{7,8},{8,9},{9,10},{10,1... | collective-permute-start | bytes 393224 | tf_op jit(solution)/shard_map/ppermute | solution.py:74
  268.5 9.0 %collective-permute-start.63 = (bf16[64,1024]{1,0:T(8,128)(2,1)S(1)}, bf16[64,1024]{1,0:T(8,128)(2,1)S(1)}, u32[]{:S(2)}, u32[]{:S(2)}) collective-permute-start(bf16[64,1024]{1,0:T(8,128)(2,1)S(1)} %collective-permute-done.61), channel_id=1, source_target_pairs={{0,15},{1,0},{2,1},{3,2},{4,3},{5,4},{6,5},{7,6},{8,7},{9,8},{10,9... | collective-permute-start | bytes 393224 | tf_op jit(solution)/shard_map/ppermute | solution.py:82
  275.6 8.1 %collective-permute-start.64 = (bf16[64,1024]{1,0:T(8,128)(2,1)S(1)}, bf16[64,1024]{1,0:T(8,128)(2,1)S(1)}, u32[]{:S(2)}, u32[]{:S(2)}) collective-permute-start(bf16[64,1024]{1,0:T(8,128)(2,1)S(1)} %collective-permute-done.62), channel_id=1, source_target_pairs={{0,1},{1,2},{2,3},{3,4},{4,5},{5,6},{6,7},{7,8},{8,9},{9,10},{10,1... | collective-permute-start | bytes 393224 | tf_op jit(solution)/shard_map/ppermute | solution.py:74
  277.5 8.1 %collective-permute-start.65 = (bf16[64,1024]{1,0:T(8,128)(2,1)S(1)}, bf16[64,1024]{1,0:T(8,128)(2,1)S(1)}, u32[]{:S(2)}, u32[]{:S(2)}) collective-permute-start(bf16[64,1024]{1,0:T(8,128)(2,1)S(1)} %collective-permute-done.63), channel_id=1, source_target_pairs={{0,15},{1,0},{2,1},{3,2},{4,3},{5,4},{6,5},{7,6},{8,7},{9,8},{10,9... | collective-permute-start | bytes 393224 | tf_op jit(solution)/shard_map/ppermute | solution.py:82
  283.7 9.2 %collective-permute-start.66 = (bf16[64,1024]{1,0:T(8,128)(2,1)S(1)}, bf16[64,1024]{1,0:T(8,128)(2,1)S(1)}, u32[]{:S(2)}, u32[]{:S(2)}) collective-permute-start(bf16[64,1024]{1,0:T(8,128)(2,1)S(1)} %collective-permute-done.64), channel_id=1, source_target_pairs={{0,1},{1,2},{2,3},{3,4},{4,5},{5,6},{6,7},{7,8},{8,9},{9,10},{10,1... | collective-permute-start | bytes 393224 | tf_op jit(solution)/shard_map/ppermute | solution.py:74
  285.6 9.2 %collective-permute-start.67 = (bf16[64,1024]{1,0:T(8,128)(2,1)S(1)}, bf16[64,1024]{1,0:T(8,128)(2,1)S(1)}, u32[]{:S(2)}, u32[]{:S(2)}) collective-permute-start(bf16[64,1024]{1,0:T(8,128)(2,1)S(1)} %collective-permute-done.65), channel_id=1, source_target_pairs={{0,15},{1,0},{2,1},{3,2},{4,3},{5,4},{6,5},{7,6},{8,7},{9,8},{10,9... | collective-permute-start | bytes 393224 | tf_op jit(solution)/shard_map/ppermute | solution.py:82
  290.9 38.4 %collective-permute-start.56 = (f32[2,2,2,32,256]{4,3,2,1,0:T(8,128)S(1)}, f32[2,2,2,32,256]{4,3,2,1,0:T(8,128)S(1)}, u32[]{:S(2)}, u32[]{:S(2)}) collective-permute-start(f32[2,2,2,32,256]{4,3,2,1,0:T(8,128)S(1)} %dynamic-slice_bitcast_fusion.1), channel_id=1, source_target_pairs={{0,32},{16,48},{32,0},{48,16},{64,96},{80,112},{96,64},{112,80},{1... | collective-permute-start | bytes 786440 | tf_op jit(solution)/shard_map/ppermute | solution.py:33
  292.9 8.1 %collective-permute-start.68 = (bf16[64,1024]{1,0:T(8,128)(2,1)S(1)}, bf16[64,1024]{1,0:T(8,128)(2,1)S(1)}, u32[]{:S(2)}, u32[]{:S(2)}) collective-permute-start(bf16[64,1024]{1,0:T(8,128)(2,1)S(1)} %collective-permute-done.66), channel_id=1, source_target_pairs={{0,1},{1,2},{2,3},{3,4},{4,5},{5,6},{6,7},{7,8},{8,9},{9,10},{10,1... | collective-permute-start | bytes 393224 | tf_op jit(solution)/shard_map/ppermute | solution.py:74
  301.0 8.1 %collective-permute-start.70 = (bf16[64,1024]{1,0:T(8,128)(2,1)S(1)}, bf16[64,1024]{1,0:T(8,128)(2,1)S(1)}, u32[]{:S(2)}, u32[]{:S(2)}) collective-permute-start(bf16[64,1024]{1,0:T(8,128)(2,1)S(1)} %collective-permute-done.68), channel_id=1, source_target_pairs={{0,1},{1,2},{2,3},{3,4},{4,5},{5,6},{6,7},{7,8},{8,9},{9,10},{10,1... | collective-permute-start | bytes 393224 | tf_op jit(solution)/shard_map/ppermute | solution.py:74
  309.0 8.1 %collective-permute-start.72 = (bf16[64,1024]{1,0:T(8,128)(2,1)S(1)}, bf16[64,1024]{1,0:T(8,128)(2,1)S(1)}, u32[]{:S(2)}, u32[]{:S(2)}) collective-permute-start(bf16[64,1024]{1,0:T(8,128)(2,1)S(1)} %collective-permute-done.70), channel_id=1, source_target_pairs={{0,1},{1,2},{2,3},{3,4},{4,5},{5,6},{6,7},{7,8},{8,9},{9,10},{10,1... | collective-permute-start | bytes 393224 | tf_op jit(solution)/shard_map/ppermute | solution.py:74
  333.1 12.5 %collective-permute-start.76 = (f32[2,2,2,40,256]{4,3,2,1,0:T(8,128)S(1)}, f32[2,2,2,40,256]{4,3,2,1,0:T(8,128)S(1)}, u32[]{:S(2)}, u32[]{:S(2)}) collective-permute-start(f32[2,2,2,40,256]{4,3,2,1,0:T(8,128)S(1)} %dynamic-slice_bitcast_fusion), channel_id=1, source_target_pairs={{0,32},{16,48},{32,0},{48,16},{64,96},{80,112},{96,64},{112,80},{1... | collective-permute-start | bytes 983048 | tf_op jit(solution)/shard_map/ppermute | solution.py:33
  337.3 11.0 %collective-permute-start.58 = (f32[2,32,256]{2,1,0:T(8,128)S(1)}, f32[2,32,256]{2,1,0:T(8,128)S(1)}, u32[]{:S(2)}, u32[]{:S(2)}) collective-permute-start(f32[2,32,256]{2,1,0:T(8,128)S(1)} %dynamic-slice_bitcast_fusion.9), channel_id=1, source_target_pairs={{0,64},{16,80},{32,96},{48,112},{64,0},{80,16},{96,32},{112,48},{1... | collective-permute-start | bytes 196616 | tf_op jit(solution)/shard_map/ppermute | solution.py:33
  352.9 10.2 %collective-permute-start.78 = (f32[2,40,256]{2,1,0:T(8,128)S(1)}, f32[2,40,256]{2,1,0:T(8,128)S(1)}, u32[]{:S(2)}, u32[]{:S(2)}) collective-permute-start(f32[2,40,256]{2,1,0:T(8,128)S(1)} %dynamic-slice_bitcast_fusion.8), channel_id=1, source_target_pairs={{0,64},{16,80},{32,96},{48,112},{64,0},{80,16},{96,32},{112,48},{1... | collective-permute-start | bytes 245768 | tf_op jit(solution)/shard_map/ppermute | solution.py:33
  (22 other events, 212.2 us)
